TPU v7x, 256 devices: a whole 4x4x8 slice. The times are simulated.
256 devices in a mesh: section: 2 (over core), expert: 32 (over x, z), dp: 4 (over y).
Axes of the slice: x: 4, y: 4, z: 8, core: 2. Of those that a mesh axis runs over, the one named last changes fastest.
Arguments:
- tokens: bfloat16 [2, 16384, 1024], P(None, ('expert', 'dp')), may hold values from -6 to 6
- cotangent: bfloat16 [2, 16384, 1024], P(None, ('expert', 'dp')), may hold values from -6 to 6
- routes: int32 [2, 2, 16384, 2], P('section', None, ('expert', 'dp')), may hold values from 0 to 31, all different within a row; in each aligned block of 128 rows (0 to 127, 128 to 255, ..., all dimensions but the last counted through in order) at most 12 rows name the same one
- router: bfloat16 [2, 1024, 32], P('section'), may hold values from -0.1875 to 0.1875
- w_gate: bfloat16 [2, 32, 1024, 512], P('section', 'expert'), may hold values from -0.1875 to 0.1875
- w_up: bfloat16 [2, 32, 1024, 512], P('section', 'expert'), may hold values from -0.1875 to 0.1875
- w_down: bfloat16 [2, 32, 512, 1024], P('section', 'expert'), may hold values from -0.25 to 0.25
Outputs:
- out_layers: bfloat16 [2, 2, 16384, 1024], P('section', None, ('expert', 'dp'))
- grad_in: bfloat16 [2, 2, 16384, 1024], P('section', None, ('expert', 'dp'))
- grad_gate: float32 [2, 32, 1024, 512], P('section', 'expert', 'dp')
- grad_up: float32 [2, 32, 1024, 512], P('section', 'expert', 'dp')
- grad_down: float32 [2, 32, 512, 1024], P('section', 'expert', 'dp')
- grad_router: float32 [2, 1024, 32], P('section')
Inputs may be any that keep to these rules, and one draw needn't show every extreme that they name: `routes`: each token names 2 different experts. Within the tokens of one device (an aligned block of 128 tokens of one layer and micro-batch) no expert is named by more than 12 tokens, and in every draw some expert is named by exactly 12 tokens of some block.
All inputs are finite; a program needn't handle non-finite values.
Results may differ from a plain program's by a relative error of at most 0.012.
Values may be sent and summed in bfloat16 or wider, within the bound.
No kernel may reach another device: no remote copies, remote signals or barrier semaphores. Data moves between devices by JAX's collectives and lax.ppermute only.
A program may use at most 128 MiB of HBM per device.

v0:
```python
import math

import jax
import jax.numpy as jnp
from jax import lax
from jax.sharding import PartitionSpec as P


def from_behind(array, axis, by):
    length = lax.axis_size(axis)
    pairs = [(i, i + by) for i in range(length) if 0 <= i + by < length]
    return lax.ppermute(array, axis, pairs)


def contract_last(left, right):
    return lax.dot_general(
        left, right, (((1,), (1,)), ((), ())), preferred_element_type=jnp.float32
    )


def contract_first(left, right):
    return lax.dot_general(
        left, right, (((0,), (0,)), ((), ())), preferred_element_type=jnp.float32
    )


def slot_index(chosen, experts, capacity):
    flat = chosen.reshape(-1)
    labels = jnp.arange(experts, dtype=jnp.int32)
    onehot = (flat[:, None] == labels[None, :]).astype(jnp.int32)
    before = jnp.cumsum(onehot, axis=0) - onehot
    position = jnp.sum(before * onehot, axis=1)
    return flat * capacity + position


def route_weights(hidden, chosen, router_layer):
    logits = jnp.dot(hidden, router_layer, preferred_element_type=jnp.float32)
    labels = jnp.arange(logits.shape[1], dtype=jnp.int32)
    match = chosen[:, :, None] == labels[None, None, :]
    picked = jnp.sum(jnp.where(match, logits[:, None, :], 0.0), axis=2)
    raised = jnp.exp(picked)
    return raised / jnp.sum(raised, axis=1, keepdims=True)


def expert_trade(block):
    return lax.all_to_all(block, "expert", split_axis=0, concat_axis=0, tiled=True)


def fetch(store, place):
    return lax.dynamic_index_in_dim(store, place, 0, keepdims=False)


def store_at(store, value, place, valid):
    previous = fetch(store, place)
    return lax.dynamic_update_index_in_dim(store, jnp.where(valid, value, previous), place, 0)


def shards(tokens, cotangent, routes, router, w_gate, w_up, w_down):
    sections = lax.axis_size("section")
    sources = lax.axis_size("expert")
    groups = lax.axis_size("dp")
    section_id = lax.axis_index("section")
    batches, per_device, width = tokens.shape
    top = routes.shape[3]
    experts = router.shape[2]
    capacity = 3 * per_device * top // (2 * experts)
    router_layer = router[0]
    gate_weight = w_gate[0, 0]
    up_weight = w_up[0, 0]
    down_weight = w_down[0, 0]
    units = gate_weight.shape[1]
    total_rows = sources * capacity
    ticks = batches + sections - 1
    chosen_all = routes[0]
    labels = jnp.arange(experts, dtype=jnp.int32)
    kept_inputs = jnp.zeros((batches, per_device, width), jnp.bfloat16)
    kept_picked = jnp.zeros((batches, per_device * top, width), jnp.bfloat16)
    kept_rows = jnp.zeros((batches, total_rows, width), jnp.bfloat16)
    outputs = jnp.zeros((batches, per_device, width), jnp.bfloat16)
    carried = jnp.zeros((per_device, width), jnp.bfloat16)
    for tick in range(ticks):
        batch_index = tick - section_id
        valid = jnp.logical_and(batch_index >= 0, batch_index < batches)
        place = jnp.clip(batch_index, 0, batches - 1)
        fresh = tokens[tick] if tick < batches else jnp.zeros((per_device, width), jnp.bfloat16)
        hidden = jnp.where(section_id == 0, fresh, carried)
        chosen = fetch(chosen_all, place)
        weights = route_weights(hidden, chosen, router_layer)
        index = slot_index(chosen, experts, capacity)
        spread = (
            jnp.zeros((experts * capacity, width), jnp.bfloat16)
            .at[index]
            .set(jnp.repeat(hidden, top, axis=0))
        )
        arrived = expert_trade(spread.reshape(experts, capacity, width)).reshape(total_rows, width)
        gate = jnp.dot(arrived, gate_weight, preferred_element_type=jnp.float32)
        up_term = jnp.dot(arrived, up_weight, preferred_element_type=jnp.float32)
        inner = (jax.nn.silu(gate) * up_term).astype(jnp.bfloat16)
        produced = jnp.dot(inner, down_weight, preferred_element_type=jnp.float32).astype(
            jnp.bfloat16
        )
        returned = expert_trade(produced.reshape(sources, capacity, width)).reshape(
            experts * capacity, width
        )
        picked = returned[index]
        blended = jnp.sum(
            weights[:, :, None] * picked.reshape(per_device, top, width).astype(jnp.float32), axis=1
        )
        mixed = (hidden.astype(jnp.float32) + blended).astype(jnp.bfloat16)
        outputs = store_at(outputs, mixed, place, valid)
        kept_inputs = store_at(kept_inputs, hidden, place, valid)
        kept_picked = store_at(kept_picked, picked, place, valid)
        kept_rows = store_at(kept_rows, arrived, place, valid)
        if tick + 1 < ticks:
            carried = from_behind(mixed, "section", 1)
    kept_dgate = jnp.zeros((batches, total_rows, units), jnp.bfloat16)
    kept_dup = jnp.zeros((batches, total_rows, units), jnp.bfloat16)
    kept_inner = jnp.zeros((batches, total_rows, units), jnp.bfloat16)
    kept_grads = jnp.zeros((batches, total_rows, width), jnp.bfloat16)
    sum_router = jnp.zeros((width, experts), jnp.float32)
    grad_store = jnp.zeros((batches, per_device, width), jnp.bfloat16)
    carried = jnp.zeros((per_device, width), jnp.bfloat16)
    for tick in range(ticks):
        batch_index = tick - (sections - 1 - section_id)
        valid = jnp.logical_and(batch_index >= 0, batch_index < batches)
        place = jnp.clip(batch_index, 0, batches - 1)
        fresh = cotangent[tick] if tick < batches else jnp.zeros((per_device, width), jnp.bfloat16)
        upstream = jnp.where(section_id == sections - 1, fresh, carried)
        upstream = jnp.where(valid, upstream, jnp.zeros_like(upstream))
        chosen = fetch(chosen_all, place)
        hidden = fetch(kept_inputs, place)
        picked = fetch(kept_picked, place)
        arrived = fetch(kept_rows, place)
        weights = route_weights(hidden, chosen, router_layer)
        index = slot_index(chosen, experts, capacity)
        flowing = upstream.astype(jnp.float32)
        along = jnp.sum(
            flowing[:, None, :] * picked.reshape(per_device, top, width).astype(jnp.float32), axis=2
        )
        grad_y = (
            (weights[:, :, None] * flowing[:, None, :])
            .astype(jnp.bfloat16)
            .reshape(per_device * top, width)
        )
        spread = jnp.zeros((experts * capacity, width), jnp.bfloat16).at[index].set(grad_y)
        grad_rows = expert_trade(spread.reshape(experts, capacity, width)).reshape(
            total_rows, width
        )
        gate = jnp.dot(arrived, gate_weight, preferred_element_type=jnp.float32)
        up_term = jnp.dot(arrived, up_weight, preferred_element_type=jnp.float32)
        active = jax.nn.silu(gate)
        inner = (active * up_term).astype(jnp.bfloat16)
        d_hidden = contract_last(grad_rows, down_weight)
        sigma = jax.nn.sigmoid(gate)
        d_gate = (d_hidden * up_term * sigma * (1.0 + gate * (1.0 - sigma))).astype(jnp.bfloat16)
        d_up = (d_hidden * active).astype(jnp.bfloat16)
        d_rows = (contract_last(d_gate, gate_weight) + contract_last(d_up, up_weight)).astype(
            jnp.bfloat16
        )
        returned = expert_trade(d_rows.reshape(sources, capacity, width)).reshape(
            experts * capacity, width
        )
        back = returned[index].reshape(per_device, top, width)
        grad_h = flowing + jnp.sum(back.astype(jnp.float32), axis=1)
        grad_s = weights * (along - jnp.sum(weights * along, axis=1, keepdims=True))
        match = chosen[:, :, None] == labels[None, None, :]
        grad_logits = jnp.sum(jnp.where(match, grad_s[:, :, None], 0.0), axis=1).astype(
            jnp.bfloat16
        )
        local_router = contract_first(hidden, grad_logits)
        grad_h = grad_h + contract_last(grad_logits, router_layer)
        passed = grad_h.astype(jnp.bfloat16)
        grad_store = store_at(grad_store, passed, place, valid)
        kept_dgate = store_at(kept_dgate, d_gate, place, valid)
        kept_dup = store_at(kept_dup, d_up, place, valid)
        kept_inner = store_at(kept_inner, inner, place, valid)
        kept_grads = store_at(kept_grads, grad_rows, place, valid)
        sum_router = sum_router + local_router
        if tick + 1 < ticks:
            carried = from_behind(passed, "section", -1)
    all_rows = kept_rows.reshape(batches * total_rows, width)
    whole_gate = contract_first(all_rows, kept_dgate.reshape(batches * total_rows, units))
    whole_up = contract_first(all_rows, kept_dup.reshape(batches * total_rows, units))
    whole_down = contract_first(
        kept_inner.reshape(batches * total_rows, units),
        kept_grads.reshape(batches * total_rows, width),
    )
    shares = (
        lax.psum_scatter(
            whole_gate.astype(jnp.bfloat16), "dp", scatter_dimension=0, tiled=True
        ).astype(jnp.float32),
        lax.psum_scatter(
            whole_up.astype(jnp.bfloat16), "dp", scatter_dimension=0, tiled=True
        ).astype(jnp.float32),
        lax.psum_scatter(
            whole_down.astype(jnp.bfloat16), "dp", scatter_dimension=0, tiled=True
        ).astype(jnp.float32),
    )
    sum_gate = shares[0]
    sum_up = shares[1]
    sum_down = shares[2]
    sum_router = lax.psum(sum_router, ("expert", "dp"))
    expert_scale = 1.0 / math.sqrt(batches * groups * per_device * top)
    router_scale = 1.0 / math.sqrt(batches * per_device * sources * groups)
    return (
        outputs[None],
        grad_store[None],
        (sum_gate * expert_scale)[None, None],
        (sum_up * expert_scale)[None, None],
        (sum_down * expert_scale)[None, None],
        (sum_router * router_scale)[None],
    )


def solution(mesh):
    placed = (
        P(None, ("expert", "dp"), None),
        P(None, ("expert", "dp"), None),
        P("section", None, ("expert", "dp"), None),
        P("section", None, None),
        P("section", "expert", None, None),
        P("section", "expert", None, None),
        P("section", "expert", None, None),
    )
    return jax.shard_map(
        shards,
        mesh=mesh,
        in_specs=placed,
        out_specs=(
            P("section", None, ("expert", "dp"), None),
            P("section", None, ("expert", "dp"), None),
            P("section", "expert", "dp", None),
            P("section", "expert", "dp", None),
            P("section", "expert", "dp", None),
            P("section", None, None),
        ),
        check_vma=False,
    )
```

profile of v0, /device:TPU:32, one launch (start us, length us, event | category | flops | bytes accessed | tf_op | source)
XLA Modules:
  0.0 837.6 jit_solution(2187735484304862792)
XLA Ops:
  18.5 39.8 %all_to_all.60 = bf16[32,12,1024]{2,1,0:T(8,128)(2,1)S(1)} all-to-all(bf16[32,12,1024]{2,1,0:T(8,128)(2,1)} %reshape.769), channel_id=1, replica_groups=mesh['section'=2,'expert'=32,'dp'=4] {'expert'}, dimensions={0} | all-to-all | bytes 1572864 | tf_op jit(solution)/shard_map/all_to_all | solution.py:46
  60.4 2.7 fusion.44
  63.1 3.4 convolution_convert_fusion.2
  68.7 5.3 all-to-all-start.1
  76.9 25.2 %all-to-all-done.1 = bf16[32,12,1024]{2,1,0:T(8,128)(2,1)} async-done(((bf16[32,12,1024]{2,1,0:T(8,128)(2,1)}), bf16[32,12,1024]{2,1,0:T(8,128)(2,1)}, u32[]{:S(2)}, u32[]{:S(2)}) %all-to-all-start.1) | async-done | bytes 786464 | tf_op jit(solution)/shard_map/all_to_all | solution.py:46
  104.1 3.7 gather_fusion
  107.8 2.7 reshape.804
  110.5 2.6 multiply_reduce_fusion.5
  124.4 3.1 scatter_custom_fusion.1
  129.7 5.3 all-to-all-start.2
  137.7 26.0 %all-to-all-done.2 = bf16[32,12,1024]{2,1,0:T(8,128)(2,1)} async-done(((bf16[32,12,1024]{2,1,0:T(8,128)(2,1)}), bf16[32,12,1024]{2,1,0:T(8,128)(2,1)}, u32[]{:S(2)}, u32[]{:S(2)}) %all-to-all-start.2) | async-done | bytes 786464 | tf_op jit(solution)/shard_map/all_to_all | solution.py:46
  165.8 2.6 fusion.42
  168.4 3.4 convolution_convert_fusion.1
  173.9 5.6 all-to-all-start.3
  198.0 9.7 %all-to-all-done.3 = bf16[32,12,1024]{2,1,0:T(8,128)(2,1)} async-done(((bf16[32,12,1024]{2,1,0:T(8,128)(2,1)}), bf16[32,12,1024]{2,1,0:T(8,128)(2,1)}, u32[]{:S(2)}, u32[]{:S(2)}) %all-to-all-start.3) | async-done | bytes 786464 | tf_op jit(solution)/shard_map/all_to_all | solution.py:46
  209.8 3.7 gather_fusion.1
  213.5 2.7 reshape.805
  216.2 2.6 multiply_reduce_fusion.4
  226.8 3.1 scatter_custom_fusion.2
  232.0 5.3 all-to-all-start.4
  237.3 28.4 %all-to-all-done.4 = bf16[32,12,1024]{2,1,0:T(8,128)(2,1)} async-done(((bf16[32,12,1024]{2,1,0:T(8,128)(2,1)}), bf16[32,12,1024]{2,1,0:T(8,128)(2,1)}, u32[]{:S(2)}, u32[]{:S(2)}) %all-to-all-start.4) | async-done | bytes 786464 | tf_op jit(solution)/shard_map/all_to_all | solution.py:46
  267.8 2.6 fusion.40
  270.4 3.4 convolution_convert_fusion
  276.0 5.3 all-to-all-start.5
  283.7 2.9 mul.359
  286.6 2.9 mul.351
  300.4 8.9 %all-to-all-done.5 = bf16[32,12,1024]{2,1,0:T(8,128)(2,1)} async-done(((bf16[32,12,1024]{2,1,0:T(8,128)(2,1)}), bf16[32,12,1024]{2,1,0:T(8,128)(2,1)}, u32[]{:S(2)}, u32[]{:S(2)}) %all-to-all-start.5) | async-done | bytes 786464 | tf_op jit(solution)/shard_map/all_to_all | solution.py:46
  311.5 3.6 gather_fusion.2
  323.9 3.4 scatter_custom_fusion.3
  329.4 5.7 all-to-all-start.6
  357.5 2.6 fusion.20
  360.1 2.6 fusion.38
  365.1 3.6 select_bitcast_fusion.1
  373.0 9.7 %all-to-all-start.7 = ((bf16[32,12,1024]{2,1,0:T(8,128)(2,1)}), bf16[32,12,1024]{2,1,0:T(8,128)(2,1)}, u32[]{:S(2)}, u32[]{:S(2)}) async-start(bf16[32,12,1024]{2,1,0:T(8,128)(2,1)} %reshape.790), calls=%async_computation.7 | async-start | bytes 2097152 | tf_op jit(solution)/shard_map/all_to_all | solution.py:46
  397.6 11.9 %all-to-all-done.7 = bf16[32,12,1024]{2,1,0:T(8,128)(2,1)} async-done(((bf16[32,12,1024]{2,1,0:T(8,128)(2,1)}), bf16[32,12,1024]{2,1,0:T(8,128)(2,1)}, u32[]{:S(2)}, u32[]{:S(2)}) %all-to-all-start.7) | async-done | bytes 786464 | tf_op jit(solution)/shard_map/all_to_all | solution.py:46
  411.5 3.7 gather_fusion.3
  415.2 2.7 reshape.808
  417.9 3.3 reduce_sum.337
  428.4 3.0 mul.376
  431.4 2.9 mul.368
  441.1 3.3 scatter_custom_fusion.4
  446.5 5.1 all-to-all-start.8
  452.8 2.6 fusion.17
  478.1 3.2 all-to-all-done.8
  483.5 4.0 fusion.94
  491.8 7.0 all-to-all-start.9
  499.3 2.6 fusion.14
  511.2 16.2 %all-to-all-done.9 = bf16[32,12,1024]{2,1,0:T(8,128)(2,1)} async-done(((bf16[32,12,1024]{2,1,0:T(8,128)(2,1)}), bf16[32,12,1024]{2,1,0:T(8,128)(2,1)}, u32[]{:S(2)}, u32[]{:S(2)}) %all-to-all-start.9) | async-done | bytes 786464 | tf_op jit(solution)/shard_map/all_to_all | solution.py:46
  529.5 3.7 gather_fusion.4
  533.2 2.6 reshape.809
  535.9 3.3 reduce_sum.346
  551.3 3.0 mul.393
  554.3 2.9 mul.385
  560.5 3.4 scatter_custom_fusion.5
  565.9 5.7 all-to-all-start.10
  594.1 2.6 select_dynamic-update-slice_fusion.1
  603.0 4.2 fusion.93
  613.0 2.7 select_dynamic-update-slice_fusion
  615.7 3.4 bitcast_convert_fusion
  622.8 3.7 bitcast_convert_fusion.1
  633.9 7.8 all-to-all-start.11
  642.1 3.5 bitcast_convert_fusion.2
  648.2 2.7 multiply_reduce_fusion.3
  652.8 161.8 %all-reduce.2.cloned.1.call-done = f32[1024,32]{0,1:T(8,128)} async-done(((f32[1024,32]{0,1:T(8,128)}), f32[1024,32]{0,1:T(8,128)}) %all-reduce.2.cloned.1.call-update) | async-done | bytes 131088 | tf_op jit(solution)/shard_map/psum | solution.py:202
  (380 shorter events, 288.3 us)
Async XLA Ops:
  8.0 55.1 %copy-start = (bf16[1,1,512,1024]{3,2,1,0:T(8,128)(2,1)S(1)}, bf16[1,1,512,1024]{3,2,1,0:T(8,128)(2,1)}, u32[]{:S(2)}) copy-start(bf16[1,1,512,1024]{3,2,1,0:T(8,128)(2,1)} %param.13) | copy-start | bytes 3145732
  8.0 5.4 copy-start.20
  9.5 3.0 copy-start.37
  9.5 125.4 %copy-start.35 = (s32[1,1,128,2]{2,3,1,0:T(2,128)}, s32[1,1,128,2]{2,3,1,0:T(2,128)S(1)}, u32[]{:S(2)}) copy-start(s32[1,1,128,2]{2,3,1,0:T(2,128)S(1)} %get-tuple-element.57) | copy-start | bytes 3076
  9.5 289.8 %copy-start.32 = (s32[1,1,128,2]{2,3,1,0:T(2,128)}, s32[1,1,128,2]{2,3,1,0:T(2,128)S(1)}, u32[]{:S(2)}) copy-start(s32[1,1,128,2]{2,3,1,0:T(2,128)S(1)} %get-tuple-element.55) | copy-start | bytes 3076
  15.5 42.9 %copy-start.49 = (s32[256,1]{0,1:T(1,128)}, s32[256,1]{0,1:T(1,128)S(1)}, u32[]{:S(2)}) copy-start(s32[256,1]{0,1:T(1,128)S(1)} %get-tuple-element.71) | copy-start | bytes 3076
  18.5 41.9 %copy-start.1 = (bf16[1,1,1024,512]{3,2,1,0:T(8,128)(2,1)S(1)}, bf16[1,1,1024,512]{3,2,1,0:T(8,128)(2,1)}, u32[]{:S(2)}) copy-start(bf16[1,1,1024,512]{3,2,1,0:T(8,128)(2,1)} %param.11) | copy-start | bytes 3145732
  60.4 2.7 copy-start.2
  66.5 7.4 copy-start.11
  68.7 33.3 %all-to-all-start.1 = ((bf16[32,12,1024]{2,1,0:T(8,128)(2,1)}), bf16[32,12,1024]{2,1,0:T(8,128)(2,1)}, u32[]{:S(2)}, u32[]{:S(2)}) async-start(bf16[32,12,1024]{2,1,0:T(8,128)(2,1)} %reshape.771), calls=%async_computation.1 | async-start | bytes 2097152 | tf_op jit(solution)/shard_map/all_to_all | solution.py:46
  114.7 2.8 collective-permute-start
  129.7 34.0 %all-to-all-start.2 = ((bf16[32,12,1024]{2,1,0:T(8,128)(2,1)}), bf16[32,12,1024]{2,1,0:T(8,128)(2,1)}, u32[]{:S(2)}, u32[]{:S(2)}) async-start(bf16[32,12,1024]{2,1,0:T(8,128)(2,1)} %reshape.775), calls=%async_computation.2 | async-start | bytes 2097152 | tf_op jit(solution)/shard_map/all_to_all | solution.py:46
  173.9 22.2 %copy-start.38 = (s32[1,1,128,2]{2,3,1,0:T(2,128)S(1)}, s32[1,1,128,2]{2,3,1,0:T(2,128)}, u32[]{:S(2)}) copy-start(s32[1,1,128,2]{2,3,1,0:T(2,128)} %copy-done.37) | copy-start | bytes 3076
  173.9 33.8 %all-to-all-start.3 = ((bf16[32,12,1024]{2,1,0:T(8,128)(2,1)}), bf16[32,12,1024]{2,1,0:T(8,128)(2,1)}, u32[]{:S(2)}, u32[]{:S(2)}) async-start(bf16[32,12,1024]{2,1,0:T(8,128)(2,1)} %reshape.777), calls=%async_computation.3 | async-start | bytes 2097152 | tf_op jit(solution)/shard_map/all_to_all | solution.py:46
  216.2 2.7 copy-start.21
  216.2 5.0 copy-start.40
  216.2 5.0 copy-start.41
  216.2 5.0 copy-start.47
  216.2 5.0 copy-start.48
  219.8 3.1 collective-permute-start.1
  221.9 4.9 copy-start.46
  232.0 33.7 %all-to-all-start.4 = ((bf16[32,12,1024]{2,1,0:T(8,128)(2,1)}), bf16[32,12,1024]{2,1,0:T(8,128)(2,1)}, u32[]{:S(2)}, u32[]{:S(2)}) async-start(bf16[32,12,1024]{2,1,0:T(8,128)(2,1)} %reshape.781), calls=%async_computation.4 | async-start | bytes 2097152 | tf_op jit(solution)/shard_map/all_to_all | solution.py:46
  276.0 33.3 %all-to-all-start.5 = ((bf16[32,12,1024]{2,1,0:T(8,128)(2,1)}), bf16[32,12,1024]{2,1,0:T(8,128)(2,1)}, u32[]{:S(2)}, u32[]{:S(2)}) async-start(bf16[32,12,1024]{2,1,0:T(8,128)(2,1)} %reshape.783), calls=%async_computation.5 | async-start | bytes 2097152 | tf_op jit(solution)/shard_map/all_to_all | solution.py:46
  292.3 3.8 copy-start.7
  315.1 2.3 copy-start.10
  329.4 33.5 %all-to-all-start.6 = ((bf16[32,12,1024]{2,1,0:T(8,128)(2,1)}), bf16[32,12,1024]{2,1,0:T(8,128)(2,1)}, u32[]{:S(2)}, u32[]{:S(2)}) async-start(bf16[32,12,1024]{2,1,0:T(8,128)(2,1)} %reshape.786), calls=%async_computation.6 | async-start | bytes 2097152 | tf_op jit(solution)/shard_map/all_to_all | solution.py:46
  346.0 1.4 copy-start.13
  370.8 12.0 %copy-start.39 = (s32[2,128]{1,0:T(2,128)S(1)}, s32[2,128]{1,0:T(2,128)}, u32[]{:S(2)}) copy-start(s32[2,128]{1,0:T(2,128)} %eq.337) | copy-start | bytes 3076
  373.0 19.1 %copy-start.30 = (s32[32,2,128]{2,0,1:T(8,128)S(1)}, s32[32,2,128]{2,0,1:T(8,128)}, u32[]{:S(2)}) copy-start(s32[32,2,128]{2,0,1:T(8,128)} %reduce-window.54) | copy-start | bytes 98308
  373.0 36.4 %all-to-all-start.7 = ((bf16[32,12,1024]{2,1,0:T(8,128)(2,1)}), bf16[32,12,1024]{2,1,0:T(8,128)(2,1)}, u32[]{:S(2)}, u32[]{:S(2)}) async-start(bf16[32,12,1024]{2,1,0:T(8,128)(2,1)} %reshape.790), calls=%async_computation.7 | async-start | bytes 2097152 | tf_op jit(solution)/shard_map/all_to_all | solution.py:46
  393.6 21.7 %copy-start.43 = (s32[256,1]{0,1:T(1,128)}, s32[256,1]{0,1:T(1,128)S(1)}, u32[]{:S(2)}) copy-start(s32[256,1]{0,1:T(1,128)S(1)} %compare_select_fusion.1) | copy-start | bytes 3076
  421.2 5.0 copy-start.23
  422.7 3.5 copy-start.8
  422.7 3.5 collective-permute-start.2
  425.5 5.9 copy-start.51
  446.5 34.8 %all-to-all-start.8 = ((bf16[32,12,1024]{2,1,0:T(8,128)(2,1)}), bf16[32,12,1024]{2,1,0:T(8,128)(2,1)}, u32[]{:S(2)}, u32[]{:S(2)}) async-start(bf16[32,12,1024]{2,1,0:T(8,128)(2,1)} %reshape.793), calls=%async_computation.8 | async-start | bytes 2097152 | tf_op jit(solution)/shard_map/all_to_all | solution.py:46
  452.8 45.9 %copy-start.44 = (f32[128,2]{0,1:T(2,128)}, f32[128,2]{0,1:T(2,128)S(1)}, u32[]{:S(2)}) copy-start(f32[128,2]{0,1:T(2,128)S(1)} %select_reduce_fusion.1) | copy-start | bytes 3076
  491.8 35.7 %all-to-all-start.9 = ((bf16[32,12,1024]{2,1,0:T(8,128)(2,1)}), bf16[32,12,1024]{2,1,0:T(8,128)(2,1)}, u32[]{:S(2)}, u32[]{:S(2)}) async-start(bf16[32,12,1024]{2,1,0:T(8,128)(2,1)} %reshape.795), calls=%async_computation.9 | async-start | bytes 2097152 | tf_op jit(solution)/shard_map/all_to_all | solution.py:46
  507.4 3.8 copy-start.33
  507.4 3.8 copy-start.34
  507.4 3.8 copy-start.52
  539.2 5.2 copy-start.12
  541.6 3.7 copy-start.24
  541.6 7.4 collective-permute-start.3
  554.3 4.7 copy-start.45
  565.9 34.9 %all-to-all-start.10 = ((bf16[32,12,1024]{2,1,0:T(8,128)(2,1)}), bf16[32,12,1024]{2,1,0:T(8,128)(2,1)}, u32[]{:S(2)}, u32[]{:S(2)}) async-start(bf16[32,12,1024]{2,1,0:T(8,128)(2,1)} %reshape.798), calls=%async_computation.10 | async-start | bytes 2097152 | tf_op jit(solution)/shard_map/all_to_all | solution.py:46
  571.6 243.0 %all-reduce.2.cloned.1.call-start = ((), (), s32[]{:S(2)}) async-start(), calls=%async_computation.18 | async-start | bytes 262144 | tf_op jit(solution)/shard_map/psum | solution.py:202
  594.1 2.6 copy-start.53
  594.1 2.6 copy-start.22
  598.5 225.6 %reduce-scatter.8.cloned.1.call-start = ((), (), s32[]{:S(2)}) async-start(), calls=%async_computation.17 | async-start | bytes 1310720 | tf_op jit(solution)/shard_map/reduce_scatter | solution.py:195
  613.0 2.7 copy-start.18
  619.1 207.0 %reduce-scatter.6.cloned.1.call-start = ((), (), s32[]{:S(2)}) async-start(), calls=%async_computation.16 | async-start | bytes 1310720 | tf_op jit(solution)/shard_map/reduce_scatter | solution.py:192
  622.8 3.7 copy-start.42
  630.3 1.7 copy-start.29
  632.6 9.3 %copy-start.15 = (bf16[2,384,512]{1,2,0:T(8,128)(2,1)S(1)}, bf16[2,384,512]{1,2,0:T(8,128)(2,1)}, u32[]{:S(2)}) copy-start(bf16[2,384,512]{1,2,0:T(8,128)(2,1)} %constant_dynamic-update-slice_fusion.8) | copy-start | bytes 2359300
  632.6 9.3 %copy-start.19 = (bf16[1,384,512]{1,2,0:T(8,128)(2,1)S(1)}, bf16[1,384,512]{1,2,0:T(8,128)(2,1)}, u32[]{:S(2)}) copy-start(bf16[1,384,512]{1,2,0:T(8,128)(2,1)} %copy.133) | copy-start | bytes 1179652
  633.9 182.3 %all-to-all-start.11 = ((bf16[32,12,1024]{2,1,0:T(8,128)(2,1)}), bf16[32,12,1024]{2,1,0:T(8,128)(2,1)}, u32[]{:S(2)}, u32[]{:S(2)}) async-start(bf16[32,12,1024]{2,1,0:T(8,128)(2,1)} %reshape.800), calls=%async_computation.11 | async-start | bytes 2097152 | tf_op jit(solution)/shard_map/all_to_all | solution.py:46
  641.7 186.2 %reduce-scatter.4.cloned.1.call-start = ((), (), s32[]{:S(2)}) async-start(), calls=%async_computation.15 | async-start | bytes 1310720 | tf_op jit(solution)/shard_map/reduce_scatter | solution.py:189
  642.1 3.7 copy-start.36
  646.6 4.3 copy-start.25
  648.2 3.7 copy-start.9
  652.0 164.2 %copy-start.26 = (bf16[1,2,128,1024]{3,2,1,0:T(8,128)(2,1)}, bf16[1,2,128,1024]{3,2,1,0:T(8,128)(2,1)S(1)}, u32[]{:S(2)}) copy-start(bf16[1,2,128,1024]{3,2,1,0:T(8,128)(2,1)S(1)} %fusion.109) | copy-start | bytes 1572868
  820.3 2.5 copy-start.27
  824.1 5.6 copy-start.28
  (9 other events, 7.6 us)
Sparse Core Ops, SparseCore 0:
  598.7 215.8 all-reduce.1
Sparse Core Ops, SparseCore 1:
  619.2 25.4 reduce-scatter.7
  647.1 26.1 reduce-scatter.5
  675.6 26.0 reduce-scatter.3
where the time goes:
time: 853 us; the launch traced here: 838 us
  waiting for transfers between devices  294 us (34%)
  local copies, waits for them, and re-layouts  234 us (27%)
  other arithmetic  102 us (12%)
  matrix products  76.8 us (9%)
  starting transfers between devices  74.6 us (9%)
  blocking collectives  39.8 us (5%)
  between operations  16.9 us (2%)
    psum x1, waiting for transfers between devices, shards(): sum_router = lax.psum(sum_router, ('expert', 'dp'))  162 us
    all_to_all x11, waiting for transfers between devices, expert_trade(): lax.all_to_all(block, 'expert', split_axis=0, concat_axis=0, tiled=True)  132 us
    all_to_all x11, starting transfers between devices, expert_trade(): lax.all_to_all(block, 'expert', split_axis=0, concat_axis=0, tiled=True)  67.6 us
    all_to_all x1, blocking collectives, expert_trade(): lax.all_to_all(block, 'expert', split_axis=0, concat_axis=0, tiled=True)  39.8 us
    dynamic_slice x22, local copies, waits for them, and re-layouts, fetch(): return lax.dynamic_index_in_dim(store, place, 0, keepdims=False)  25.3 us
    dot_general x12, matrix products, contract_last(): lax.dot_general(left, right, (((1,), (1,)), ((), ())), preferred_element_...  23.4 us
    dynamic_update_slice x12, other arithmetic, store_at(): lax.dynamic_update_index_in_dim(store, jnp.where(valid, value, previous),...  22.2 us
    mul x9, local copies, waits for them, and re-layouts, shards(): weights[:, :, None] * flowing[:, None, :]  21.8 us
  transfers between devices with their start and end apart: 19, of which 11 were waited for; matrix products, arithmetic and copies ran while one was open for 26% of the time, Pallas kernels for 0%

commit v1 on v0

--- a/solution.py
+++ b/solution.py
@@ -53,6 +53,29 @@
 def store_at(store, value, place, valid):
     previous = fetch(store, place)
     return lax.dynamic_update_index_in_dim(store, jnp.where(valid, value, previous), place, 0)
+
+
+def group_reduce(whole_gate, whole_up, whole_down, groups):
+    stacked = jnp.stack(
+        [part.reshape(groups, -1) for part in (whole_gate, whole_up, whole_down)], axis=1
+    ).astype(jnp.bfloat16)
+    traded = lax.all_to_all(stacked, "dp", 0, 0, tiled=True)
+    summed = jnp.sum(traded.astype(jnp.float32), axis=0)
+    rows_gate = whole_gate.shape[0] // groups
+    rows_down = whole_down.shape[0] // groups
+    return (
+        summed[0].reshape(rows_gate, whole_gate.shape[1]),
+        summed[1].reshape(rows_gate, whole_up.shape[1]),
+        summed[2].reshape(rows_down, whole_down.shape[1]),
+    )
+
+
+def device_reduce(value, count):
+    chunks = value.reshape(count, -1, value.shape[1])
+    traded = lax.all_to_all(chunks, ("expert", "dp"), 0, 0, tiled=True)
+    total = jnp.sum(traded, axis=0, keepdims=True)
+    spread = jnp.broadcast_to(total, chunks.shape)
+    return lax.all_to_all(spread, ("expert", "dp"), 0, 0, tiled=True).reshape(value.shape)
 
 
 def shards(tokens, cotangent, routes, router, w_gate, w_up, w_down):
@@ -185,21 +208,8 @@
         kept_inner.reshape(batches * total_rows, units),
         kept_grads.reshape(batches * total_rows, width),
     )
-    shares = (
-        lax.psum_scatter(
-            whole_gate.astype(jnp.bfloat16), "dp", scatter_dimension=0, tiled=True
-        ).astype(jnp.float32),
-        lax.psum_scatter(
-            whole_up.astype(jnp.bfloat16), "dp", scatter_dimension=0, tiled=True
-        ).astype(jnp.float32),
-        lax.psum_scatter(
-            whole_down.astype(jnp.bfloat16), "dp", scatter_dimension=0, tiled=True
-        ).astype(jnp.float32),
-    )
-    sum_gate = shares[0]
-    sum_up = shares[1]
-    sum_down = shares[2]
-    sum_router = lax.psum(sum_router, ("expert", "dp"))
+    sum_gate, sum_up, sum_down = group_reduce(whole_gate, whole_up, whole_down, groups)
+    sum_router = device_reduce(sum_router, sources * groups)
     expert_scale = 1.0 / math.sqrt(batches * groups * per_device * top)
     router_scale = 1.0 / math.sqrt(batches * per_device * sources * groups)
     return (

time: 853 us -> 808 us (0.947)
  waiting for transfers between devices: 294 us -> 171 us
  blocking collectives: 39.8 us -> 73.3 us
  starting transfers between devices: 74.6 us -> 99.9 us
  local copies, waits for them, and re-layouts: 234 us -> 256 us
  between operations: 16.9 us -> 1.94 us
  other arithmetic: 102 us -> 116 us
    psum x1 -> x0, waiting for transfers between devices: 162 us -> none  [shards(): sum_router = lax.psum(sum_router, ('expert', 'dp'))]
    all_to_all x1 -> x2, blocking collectives: 39.8 us -> 73.3 us  [expert_trade(): lax.all_to_all(block, 'expert', split_axis=0, concat_axis=0, tiled=True)]
    all_to_all x0 -> x3, waiting for transfers between devices: none -> 31.5 us  [the longest x1 30.6 us: group_reduce(): traded = lax.all_to_all(stacked, 'dp', 0, 0, tiled=True)]
    all_to_all x0 -> x3, starting transfers between devices: none -> 28.8 us  [the longest x1 13.8 us: device_reduce(): lax.all_to_all(spread, ('expert', 'dp'), 0, 0, tiled=True)]
    another operation x19 -> x22, local copies, waits for them, and re-layouts: 11.3 us -> 18.9 us  [the longest x3 11.4 us: group_reduce(): jnp.stack([part.reshape(groups, -1) for part in (whole_gate, whole_up, wh...]
    all_to_all x11 -> x10, waiting for transfers between devices: 132 us -> 139 us  [expert_trade(): lax.all_to_all(block, 'expert', split_axis=0, concat_axis=0, tiled=True)]
    all_to_all x11 -> x10, starting transfers between devices: 67.6 us -> 65.1 us  [expert_trade(): lax.all_to_all(block, 'expert', split_axis=0, concat_axis=0, tiled=True)]
  transfers between devices with their start and end apart: 19 -> 17, of which waited for: 11 -> 13; matrix products, arithmetic and copies ran while one was open for 26% -> 31% of each run, Pallas kernels for 0% -> 0%
where the time goes in v1:
time: 808 us; the launch traced here: 794 us
  local copies, waits for them, and re-layouts  256 us (32%)
  waiting for transfers between devices  171 us (21%)
  other arithmetic  116 us (14%)
  starting transfers between devices  99.9 us (12%)
  matrix products  76.1 us (9%)
  blocking collectives  73.3 us (9%)
    all_to_all x10, waiting for transfers between devices, expert_trade(): lax.all_to_all(block, 'expert', split_axis=0, concat_axis=0, tiled=True)  139 us
    all_to_all x2, blocking collectives, expert_trade(): lax.all_to_all(block, 'expert', split_axis=0, concat_axis=0, tiled=True)  73.3 us
    all_to_all x10, starting transfers between devices, expert_trade(): lax.all_to_all(block, 'expert', split_axis=0, concat_axis=0, tiled=True)  65.1 us
    all_to_all x1, waiting for transfers between devices, group_reduce(): traded = lax.all_to_all(stacked, 'dp', 0, 0, tiled=True)  30.6 us
    dynamic_slice x22, local copies, waits for them, and re-layouts, fetch(): return lax.dynamic_index_in_dim(store, place, 0, keepdims=False)  25.3 us
    dot_general x12, matrix products, contract_last(): lax.dot_general(left, right, (((1,), (1,)), ((), ())), preferred_element_...  23.2 us
    dynamic_update_slice x12, other arithmetic, store_at(): lax.dynamic_update_index_in_dim(store, jnp.where(valid, value, previous),...  22.1 us
    mul x9, local copies, waits for them, and re-layouts, shards(): weights[:, :, None] * flowing[:, None, :]  21.9 us
  transfers between devices with their start and end apart: 17, of which 13 were waited for; matrix products, arithmetic and copies ran while one was open for 31% of the time, Pallas kernels for 0%

profile of v1, /device:TPU:32, one launch (start us, length us, event | category | flops | bytes accessed | tf_op | source)
XLA Modules:
  0.0 793.9 jit_solution(9707006939756197477)
XLA Ops:
  11.2 39.8 %all_to_all.75 = bf16[32,12,1024]{2,1,0:T(8,128)(2,1)S(1)} all-to-all(bf16[32,12,1024]{2,1,0:T(8,128)(2,1)} %reshape.822), channel_id=1, replica_groups=mesh['section'=2,'expert'=32,'dp'=4] {'expert'}, dimensions={0} | all-to-all | bytes 1572864 | tf_op jit(solution)/shard_map/all_to_all | solution.py:46
  53.0 2.7 fusion.44
  55.7 3.4 convolution_convert_fusion.2
  61.3 5.3 all-to-all-start.1
  69.4 25.2 %all-to-all-done.1 = bf16[32,12,1024]{2,1,0:T(8,128)(2,1)} async-done(((bf16[32,12,1024]{2,1,0:T(8,128)(2,1)}), bf16[32,12,1024]{2,1,0:T(8,128)(2,1)}, u32[]{:S(2)}, u32[]{:S(2)}) %all-to-all-start.1) | async-done | bytes 786464 | tf_op jit(solution)/shard_map/all_to_all | solution.py:46
  96.7 3.7 gather_fusion
  100.4 2.7 reshape.858
  116.8 3.1 scatter_custom_fusion.1
  122.1 5.3 all-to-all-start.2
  130.2 26.0 %all-to-all-done.2 = bf16[32,12,1024]{2,1,0:T(8,128)(2,1)} async-done(((bf16[32,12,1024]{2,1,0:T(8,128)(2,1)}), bf16[32,12,1024]{2,1,0:T(8,128)(2,1)}, u32[]{:S(2)}, u32[]{:S(2)}) %all-to-all-start.2) | async-done | bytes 786464 | tf_op jit(solution)/shard_map/all_to_all | solution.py:46
  160.8 3.4 convolution_convert_fusion.1
  166.3 5.8 all-to-all-start.3
  190.7 9.7 %all-to-all-done.3 = bf16[32,12,1024]{2,1,0:T(8,128)(2,1)} async-done(((bf16[32,12,1024]{2,1,0:T(8,128)(2,1)}), bf16[32,12,1024]{2,1,0:T(8,128)(2,1)}, u32[]{:S(2)}, u32[]{:S(2)}) %all-to-all-start.3) | async-done | bytes 786464 | tf_op jit(solution)/shard_map/all_to_all | solution.py:46
  202.5 3.7 gather_fusion.1
  206.2 2.7 reshape.859
  219.7 3.1 scatter_custom_fusion.2
  225.0 33.5 %all_to_all.76 = bf16[32,12,1024]{2,1,0:T(8,128)(2,1)} all-to-all(bf16[32,12,1024]{2,1,0:T(8,128)(2,1)} %reshape.834), channel_id=1, replica_groups=mesh['section'=2,'expert'=32,'dp'=4] {'expert'}, dimensions={0} | all-to-all | bytes 1572864 | tf_op jit(solution)/shard_map/all_to_all | solution.py:46
  263.2 3.4 convolution_convert_fusion
  268.8 5.2 all-to-all-start.5
  276.4 2.9 mul.397
  279.4 3.0 mul.389
  289.1 13.0 %all-to-all-done.5 = bf16[32,12,1024]{2,1,0:T(8,128)(2,1)} async-done(((bf16[32,12,1024]{2,1,0:T(8,128)(2,1)}), bf16[32,12,1024]{2,1,0:T(8,128)(2,1)}, u32[]{:S(2)}, u32[]{:S(2)}) %all-to-all-start.5) | async-done | bytes 786464 | tf_op jit(solution)/shard_map/all_to_all | solution.py:46
  304.3 3.6 gather_fusion.2
  313.7 3.3 scatter_custom_fusion.3
  319.2 5.6 all-to-all-start.6
  345.8 6.8 all-to-all-done.6
  354.8 3.6 select_bitcast_fusion.1
  362.6 5.3 all-to-all-start.7
  376.7 19.3 %all-to-all-done.7 = bf16[32,12,1024]{2,1,0:T(8,128)(2,1)} async-done(((bf16[32,12,1024]{2,1,0:T(8,128)(2,1)}), bf16[32,12,1024]{2,1,0:T(8,128)(2,1)}, u32[]{:S(2)}, u32[]{:S(2)}) %all-to-all-start.7) | async-done | bytes 786464 | tf_op jit(solution)/shard_map/all_to_all | solution.py:46
  398.1 3.6 gather_fusion.3
  401.7 2.7 reshape.862
  404.3 3.3 reduce_sum.355
  414.7 3.0 mul.414
  417.7 2.9 mul.406
  427.5 3.4 scatter_custom_fusion.4
  432.9 5.2 all-to-all-start.8
  464.5 3.1 all-to-all-done.8
  469.6 4.0 fusion.97
  477.9 7.4 all-to-all-start.9
  497.4 16.4 %all-to-all-done.9 = bf16[32,12,1024]{2,1,0:T(8,128)(2,1)} async-done(((bf16[32,12,1024]{2,1,0:T(8,128)(2,1)}), bf16[32,12,1024]{2,1,0:T(8,128)(2,1)}, u32[]{:S(2)}, u32[]{:S(2)}) %all-to-all-start.9) | async-done | bytes 786464 | tf_op jit(solution)/shard_map/all_to_all | solution.py:46
  515.9 3.6 gather_fusion.4
  519.5 2.8 reshape.863
  522.3 3.3 reduce_sum.364
  534.1 3.0 mul.431
  545.2 9.9 %all-to-all-start.13 = ((f32[128,1,256]{2,1,0:T(1,128)}), f32[128,1,256]{2,1,0:T(1,128)}, u32[]{:S(2)}, u32[]{:S(2)}) async-start(f32[128,1,256]{2,1,0:T(1,128)} %reshape.999), calls=%async_computation.13 | async-start | bytes 262144 | tf_op jit(solution)/shard_map/all_to_all | solution.py:75
  557.8 3.0 mul.423
  561.0 3.4 scatter_custom_fusion.5
  567.4 9.7 %all-to-all-start.10 = ((bf16[32,12,1024]{2,1,0:T(8,128)(2,1)}), bf16[32,12,1024]{2,1,0:T(8,128)(2,1)}, u32[]{:S(2)}, u32[]{:S(2)}) async-start(bf16[32,12,1024]{2,1,0:T(8,128)(2,1)} %reshape.851), calls=%async_computation.10 | async-start | bytes 2097152 | tf_op jit(solution)/shard_map/all_to_all | solution.py:46
  620.8 13.8 %all-to-all-start.14 = ((f32[128,1,256]{2,1,0:T(1,128)}), f32[128,1,256]{2,1,0:T(1,128)}, u32[]{:S(2)}, u32[]{:S(2)}) async-start(f32[128,1,256]{2,1,0:T(1,128)} %reshape.1001), calls=%async_computation.14 | async-start | bytes 262144 | tf_op jit(solution)/shard_map/all_to_all | solution.py:78
  636.8 4.2 fusion.96
  644.8 3.6 bitcast_convert_fusion.2
  648.4 3.8 stack_reshape.15
  655.8 3.6 bitcast_convert_fusion.1
  659.4 3.8 stack_reshape.16
  671.6 3.4 bitcast_convert_fusion
  675.0 3.9 stack_reshape.17
  684.4 10.3 %all-to-all-start.11 = ((bf16[32,12,1024]{2,1,0:T(8,128)(2,1)}), bf16[32,12,1024]{2,1,0:T(8,128)(2,1)}, u32[]{:S(2)}, u32[]{:S(2)}) async-start(bf16[32,12,1024]{2,1,0:T(8,128)(2,1)} %reshape.853), calls=%async_computation.11 | async-start | bytes 2097152 | tf_op jit(solution)/shard_map/all_to_all | solution.py:46
  694.6 9.4 %pad_maximum_fusion = bf16[4,3,131072]{2,1,0:T(4,128)(2,1)} fusion(bf16[4,1,131072]{2,1,0:T(2,128)(2,1)} %stack_reshape.17, bf16[4,1,131072]{2,1,0:T(2,128)(2,1)} %stack_reshape.16, bf16[4,1,131072]{2,1,0:T(2,128)(2,1)S(1)} %copy-done.4), kind=kLoop, calls=%fused_computation.13 | loop fusion | flops 9437184 | bytes 6291456 | tf_op jit(solution)/shard_map/stack | solution.py:59
  704.1 19.3 %all-to-all-done.11 = bf16[32,12,1024]{2,1,0:T(8,128)(2,1)} async-done(((bf16[32,12,1024]{2,1,0:T(8,128)(2,1)}), bf16[32,12,1024]{2,1,0:T(8,128)(2,1)}, u32[]{:S(2)}, u32[]{:S(2)}) %all-to-all-start.11) | async-done | bytes 786464 | tf_op jit(solution)/shard_map/all_to_all | solution.py:46
  723.3 5.1 all-to-all-start.12
  731.5 2.7 multiply_reduce_fusion.3
  746.7 30.6 %all-to-all-done.12 = bf16[4,3,131072]{2,1,0:T(4,128)(2,1)} async-done(((bf16[4,3,131072]{2,1,0:T(4,128)(2,1)}), bf16[4,3,131072]{2,1,0:T(4,128)(2,1)}, u32[]{:S(2)}, u32[]{:S(2)}) %all-to-all-start.12) | async-done | bytes 3145760 | tf_op jit(solution)/shard_map/all_to_all | solution.py:62
  777.3 4.7 convert_reduce_fusion
  782.0 6.7 fusion.79
  (372 shorter events, 315.5 us)
Async XLA Ops:
  0.6 55.1 %copy-start = (bf16[1,1,512,1024]{3,2,1,0:T(8,128)(2,1)S(1)}, bf16[1,1,512,1024]{3,2,1,0:T(8,128)(2,1)}, u32[]{:S(2)}) copy-start(bf16[1,1,512,1024]{3,2,1,0:T(8,128)(2,1)} %param.13) | copy-start | bytes 3145732
  0.6 5.4 copy-start.20
  2.2 3.0 copy-start.33
  2.2 125.2 %copy-start.31 = (s32[1,1,128,2]{2,3,1,0:T(2,128)}, s32[1,1,128,2]{2,3,1,0:T(2,128)S(1)}, u32[]{:S(2)}) copy-start(s32[1,1,128,2]{2,3,1,0:T(2,128)S(1)} %get-tuple-element.78) | copy-start | bytes 3076
  2.2 286.4 %copy-start.30 = (s32[1,1,128,2]{2,3,1,0:T(2,128)}, s32[1,1,128,2]{2,3,1,0:T(2,128)S(1)}, u32[]{:S(2)}) copy-start(s32[1,1,128,2]{2,3,1,0:T(2,128)S(1)} %get-tuple-element.76) | copy-start | bytes 3076
  8.1 42.9 %copy-start.42 = (s32[256,1]{0,1:T(1,128)}, s32[256,1]{0,1:T(1,128)S(1)}, u32[]{:S(2)}) copy-start(s32[256,1]{0,1:T(1,128)S(1)} %get-tuple-element.92) | copy-start | bytes 3076
  11.2 41.9 %copy-start.1 = (bf16[1,1,1024,512]{3,2,1,0:T(8,128)(2,1)S(1)}, bf16[1,1,1024,512]{3,2,1,0:T(8,128)(2,1)}, u32[]{:S(2)}) copy-start(bf16[1,1,1024,512]{3,2,1,0:T(8,128)(2,1)} %param.11) | copy-start | bytes 3145732
  51.0 1.0 copy-start.3
  53.0 2.7 copy-start.2
  59.1 7.4 copy-start.12
  61.3 33.3 %all-to-all-start.1 = ((bf16[32,12,1024]{2,1,0:T(8,128)(2,1)}), bf16[32,12,1024]{2,1,0:T(8,128)(2,1)}, u32[]{:S(2)}, u32[]{:S(2)}) async-start(bf16[32,12,1024]{2,1,0:T(8,128)(2,1)} %reshape.824), calls=%async_computation.1 | async-start | bytes 2097152 | tf_op jit(solution)/shard_map/all_to_all | solution.py:46
  105.7 0.8 copy-start.6
  107.3 2.6 collective-permute-start
  110.0 0.7 copy-start.29
  122.1 34.0 %all-to-all-start.2 = ((bf16[32,12,1024]{2,1,0:T(8,128)(2,1)}), bf16[32,12,1024]{2,1,0:T(8,128)(2,1)}, u32[]{:S(2)}, u32[]{:S(2)}) async-start(bf16[32,12,1024]{2,1,0:T(8,128)(2,1)} %reshape.828), calls=%async_computation.2 | async-start | bytes 2097152 | tf_op jit(solution)/shard_map/all_to_all | solution.py:46
  166.3 22.5 %copy-start.34 = (s32[1,1,128,2]{2,3,1,0:T(2,128)S(1)}, s32[1,1,128,2]{2,3,1,0:T(2,128)}, u32[]{:S(2)}) copy-start(s32[1,1,128,2]{2,3,1,0:T(2,128)} %copy-done.33) | copy-start | bytes 3076
  166.3 34.1 %all-to-all-start.3 = ((bf16[32,12,1024]{2,1,0:T(8,128)(2,1)}), bf16[32,12,1024]{2,1,0:T(8,128)(2,1)}, u32[]{:S(2)}, u32[]{:S(2)}) async-start(bf16[32,12,1024]{2,1,0:T(8,128)(2,1)} %reshape.830), calls=%async_computation.3 | async-start | bytes 2097152 | tf_op jit(solution)/shard_map/all_to_all | solution.py:46
  209.0 2.7 copy-start.21
  209.0 5.2 copy-start.35
  209.0 5.2 copy-start.36
  209.0 5.3 copy-start.40
  209.0 5.3 copy-start.41
  212.5 3.3 collective-permute-start.1
  268.8 33.3 %all-to-all-start.5 = ((bf16[32,12,1024]{2,1,0:T(8,128)(2,1)}), bf16[32,12,1024]{2,1,0:T(8,128)(2,1)}, u32[]{:S(2)}, u32[]{:S(2)}) async-start(bf16[32,12,1024]{2,1,0:T(8,128)(2,1)} %reshape.836), calls=%async_computation.5 | async-start | bytes 2097152 | tf_op jit(solution)/shard_map/all_to_all | solution.py:46
  282.3 3.1 copy-start.8
  288.6 19.3 %copy-start.43 = (f32[128,2]{0,1:T(2,128)}, f32[128,2]{0,1:T(2,128)S(1)}, u32[]{:S(2)}) copy-start(f32[128,2]{0,1:T(2,128)S(1)} %select_reduce_fusion.5) | copy-start | bytes 3076
  307.9 2.3 copy-start.11
  319.2 33.5 %all-to-all-start.6 = ((bf16[32,12,1024]{2,1,0:T(8,128)(2,1)}), bf16[32,12,1024]{2,1,0:T(8,128)(2,1)}, u32[]{:S(2)}, u32[]{:S(2)}) async-start(bf16[32,12,1024]{2,1,0:T(8,128)(2,1)} %reshape.839), calls=%async_computation.6 | async-start | bytes 2097152 | tf_op jit(solution)/shard_map/all_to_all | solution.py:46
  329.2 1.4 copy-start.14
  362.6 33.3 %all-to-all-start.7 = ((bf16[32,12,1024]{2,1,0:T(8,128)(2,1)}), bf16[32,12,1024]{2,1,0:T(8,128)(2,1)}, u32[]{:S(2)}, u32[]{:S(2)}) async-start(bf16[32,12,1024]{2,1,0:T(8,128)(2,1)} %reshape.843), calls=%async_computation.7 | async-start | bytes 2097152 | tf_op jit(solution)/shard_map/all_to_all | solution.py:46
  407.6 4.9 copy-start.24
  409.1 3.3 copy-start.9
  409.1 3.4 collective-permute-start.2
  411.8 5.9 copy-start.44
  412.6 0.8 copy-start.5
  432.9 34.6 %all-to-all-start.8 = ((bf16[32,12,1024]{2,1,0:T(8,128)(2,1)}), bf16[32,12,1024]{2,1,0:T(8,128)(2,1)}, u32[]{:S(2)}, u32[]{:S(2)}) async-start(bf16[32,12,1024]{2,1,0:T(8,128)(2,1)} %reshape.846), calls=%async_computation.8 | async-start | bytes 2097152 | tf_op jit(solution)/shard_map/all_to_all | solution.py:46
  447.3 0.9 copy-start.15
  454.1 0.9 copy-start.16
  460.8 0.9 copy-start.17
  477.9 35.9 %all-to-all-start.9 = ((bf16[32,12,1024]{2,1,0:T(8,128)(2,1)}), bf16[32,12,1024]{2,1,0:T(8,128)(2,1)}, u32[]{:S(2)}, u32[]{:S(2)}) async-start(bf16[32,12,1024]{2,1,0:T(8,128)(2,1)} %reshape.848), calls=%async_computation.9 | async-start | bytes 2097152 | tf_op jit(solution)/shard_map/all_to_all | solution.py:46
  494.4 25.1 %copy-start.38 = (f32[128,2]{0,1:T(2,128)}, f32[128,2]{0,1:T(2,128)S(1)}, u32[]{:S(2)}) copy-start(f32[128,2]{0,1:T(2,128)S(1)} %select_reduce_fusion.1) | copy-start | bytes 3076
  527.8 4.2 collective-permute-start.3
  532.0 0.7 copy-start.22
  534.0 4.8 copy-start.39
  545.2 22.2 %all-to-all-start.13 = ((f32[128,1,256]{2,1,0:T(1,128)}), f32[128,1,256]{2,1,0:T(1,128)}, u32[]{:S(2)}, u32[]{:S(2)}) async-start(f32[128,1,256]{2,1,0:T(1,128)} %reshape.999), calls=%async_computation.13 | async-start | bytes 262144 | tf_op jit(solution)/shard_map/all_to_all | solution.py:75
  557.8 3.1 copy-start.37
  567.4 53.4 %all-to-all-start.10 = ((bf16[32,12,1024]{2,1,0:T(8,128)(2,1)}), bf16[32,12,1024]{2,1,0:T(8,128)(2,1)}, u32[]{:S(2)}, u32[]{:S(2)}) async-start(bf16[32,12,1024]{2,1,0:T(8,128)(2,1)} %reshape.851), calls=%async_computation.10 | async-start | bytes 2097152 | tf_op jit(solution)/shard_map/all_to_all | solution.py:46
  582.9 1.3 copy-start.13
  620.8 63.5 %all-to-all-start.14 = ((f32[128,1,256]{2,1,0:T(1,128)}), f32[128,1,256]{2,1,0:T(1,128)}, u32[]{:S(2)}, u32[]{:S(2)}) async-start(f32[128,1,256]{2,1,0:T(1,128)} %reshape.1001), calls=%async_computation.14 | async-start | bytes 262144 | tf_op jit(solution)/shard_map/all_to_all | solution.py:78
  669.0 2.6 copy-start.18
  678.9 1.7 copy-start.28
  682.1 12.6 %copy-start.4 = (bf16[4,1,131072]{2,1,0:T(2,128)(2,1)S(1)}, bf16[4,1,131072]{2,1,0:T(2,128)(2,1)}, u32[]{:S(2)}) copy-start(bf16[4,1,131072]{2,1,0:T(2,128)(2,1)} %stack_reshape.15) | copy-start | bytes 3145732
  684.4 39.0 %all-to-all-start.11 = ((bf16[32,12,1024]{2,1,0:T(8,128)(2,1)}), bf16[32,12,1024]{2,1,0:T(8,128)(2,1)}, u32[]{:S(2)}, u32[]{:S(2)}) async-start(bf16[32,12,1024]{2,1,0:T(8,128)(2,1)} %reshape.853), calls=%async_computation.11 | async-start | bytes 2097152 | tf_op jit(solution)/shard_map/all_to_all | solution.py:46
  704.1 25.6 %copy-start.32 = (s32[1,1,128,2]{2,3,1,0:T(2,128)S(1)}, s32[1,1,128,2]{2,3,1,0:T(2,128)}, u32[]{:S(2)}) copy-start(s32[1,1,128,2]{2,3,1,0:T(2,128)} %copy-done.31) | copy-start | bytes 3076
  723.3 54.0 %all-to-all-start.12 = ((bf16[4,3,131072]{2,1,0:T(4,128)(2,1)}), bf16[4,3,131072]{2,1,0:T(4,128)(2,1)}, u32[]{:S(2)}, u32[]{:S(2)}) async-start(bf16[4,3,131072]{2,1,0:T(4,128)(2,1)} %pad_maximum_fusion), calls=%async_computation.12 | async-start | bytes 8388608 | tf_op jit(solution)/shard_map/all_to_all | solution.py:62
  728.4 1.5 copy-start.7
  731.5 3.7 copy-start.10
  735.3 2.6 copy-start.27
  741.4 4.2 copy-start.23
  743.1 2.5 copy-start.25
  745.9 0.8 copy-start.26
  788.7 3.9 copy-start.19

commit v2 on v1

v2 whole, which is shorter than its diff:
```python
import math

import jax
import jax.numpy as jnp
from jax import lax
from jax.sharding import PartitionSpec as P


def from_behind(array, axis, by):
    length = lax.axis_size(axis)
    pairs = [(i, i + by) for i in range(length) if 0 <= i + by < length]
    return lax.ppermute(array, axis, pairs)


def contract_last(left, right):
    return lax.dot_general(
        left, right, (((1,), (1,)), ((), ())), preferred_element_type=jnp.float32
    )


def contract_first(left, right):
    return lax.dot_general(
        left, right, (((0,), (0,)), ((), ())), preferred_element_type=jnp.float32
    )


def slot_index(chosen, experts, capacity):
    flat = chosen.reshape(-1)
    labels = jnp.arange(experts, dtype=jnp.int32)
    onehot = (flat[:, None] == labels[None, :]).astype(jnp.int32)
    before = jnp.cumsum(onehot, axis=0) - onehot
    position = jnp.sum(before * onehot, axis=1)
    return flat * capacity + position


def route_weights(hidden, chosen, router_layer):
    logits = jnp.dot(hidden, router_layer, preferred_element_type=jnp.float32)
    labels = jnp.arange(logits.shape[1], dtype=jnp.int32)
    match = chosen[:, :, None] == labels[None, None, :]
    picked = jnp.sum(jnp.where(match, logits[:, None, :], 0.0), axis=2)
    raised = jnp.exp(picked)
    return raised / jnp.sum(raised, axis=1, keepdims=True)


def expert_trade(block):
    return lax.all_to_all(block, "expert", split_axis=0, concat_axis=0, tiled=True)


def fetch(store, place):
    return lax.dynamic_index_in_dim(store, place, 0, keepdims=False)


def store_at(store, value, place, valid):
    previous = fetch(store, place)
    return lax.dynamic_update_index_in_dim(store, jnp.where(valid, value, previous), place, 0)


def group_reduce(whole_gate, whole_up, whole_down, groups):
    stacked = jnp.stack(
        [part.reshape(groups, -1) for part in (whole_gate, whole_up, whole_down)], axis=1
    ).astype(jnp.bfloat16)
    traded = lax.all_to_all(stacked, "dp", 0, 0, tiled=True)
    summed = jnp.sum(traded.astype(jnp.float32), axis=0)
    rows_gate = whole_gate.shape[0] // groups
    rows_down = whole_down.shape[0] // groups
    return (
        summed[0].reshape(rows_gate, whole_gate.shape[1]),
        summed[1].reshape(rows_gate, whole_up.shape[1]),
        summed[2].reshape(rows_down, whole_down.shape[1]),
    )


def device_reduce(value, count):
    chunks = value.reshape(count, -1, value.shape[1])
    traded = lax.all_to_all(chunks, ("expert", "dp"), 0, 0, tiled=True)
    total = jnp.sum(traded, axis=0, keepdims=True)
    spread = jnp.broadcast_to(total, chunks.shape)
    return lax.all_to_all(spread, ("expert", "dp"), 0, 0, tiled=True).reshape(value.shape)


def swap(array):
    return lax.ppermute(array, "section", [(0, 1), (1, 0)])


def pick(flag, first, second):
    return jnp.where(flag, first, second)


def layer_forward(hidden, chosen, router_layer, gate_weight, up_weight, down_weight, shape):
    experts, capacity, sources, width = shape
    per_device = hidden.shape[0]
    top = chosen.shape[1]
    weights = route_weights(hidden, chosen, router_layer)
    index = slot_index(chosen, experts, capacity)
    spread = (
        jnp.zeros((experts * capacity, width), jnp.bfloat16)
        .at[index]
        .set(jnp.repeat(hidden, top, axis=0))
    )
    arrived = expert_trade(spread.reshape(experts, capacity, width)).reshape(
        sources * capacity, width
    )
    gate = jnp.dot(arrived, gate_weight, preferred_element_type=jnp.float32)
    up_term = jnp.dot(arrived, up_weight, preferred_element_type=jnp.float32)
    inner = (jax.nn.silu(gate) * up_term).astype(jnp.bfloat16)
    produced = jnp.dot(inner, down_weight, preferred_element_type=jnp.float32).astype(jnp.bfloat16)
    returned = expert_trade(produced.reshape(sources, capacity, width)).reshape(
        experts * capacity, width
    )
    picked = returned[index]
    blended = jnp.sum(
        weights[:, :, None] * picked.reshape(per_device, top, width).astype(jnp.float32), axis=1
    )
    mixed = (hidden.astype(jnp.float32) + blended).astype(jnp.bfloat16)
    return mixed, (hidden, picked, arrived, weights, index)


def layer_backward(upstream, saved, chosen, router_layer, gate_weight, up_weight, down_weight, shape):
    experts, capacity, sources, width = shape
    hidden, picked, arrived, weights, index = saved
    per_device = hidden.shape[0]
    top = chosen.shape[1]
    labels = jnp.arange(experts, dtype=jnp.int32)
    flowing = upstream.astype(jnp.float32)
    along = jnp.sum(
        flowing[:, None, :] * picked.reshape(per_device, top, width).astype(jnp.float32), axis=2
    )
    grad_y = (
        (weights[:, :, None] * flowing[:, None, :])
        .astype(jnp.bfloat16)
        .reshape(per_device * top, width)
    )
    spread = jnp.zeros((experts * capacity, width), jnp.bfloat16).at[index].set(grad_y)
    grad_rows = expert_trade(spread.reshape(experts, capacity, width)).reshape(
        sources * capacity, width
    )
    gate = jnp.dot(arrived, gate_weight, preferred_element_type=jnp.float32)
    up_term = jnp.dot(arrived, up_weight, preferred_element_type=jnp.float32)
    active = jax.nn.silu(gate)
    inner = (active * up_term).astype(jnp.bfloat16)
    d_hidden = contract_last(grad_rows, down_weight)
    sigma = jax.nn.sigmoid(gate)
    d_gate = (d_hidden * up_term * sigma * (1.0 + gate * (1.0 - sigma))).astype(jnp.bfloat16)
    d_up = (d_hidden * active).astype(jnp.bfloat16)
    d_rows = (contract_last(d_gate, gate_weight) + contract_last(d_up, up_weight)).astype(
        jnp.bfloat16
    )
    returned = expert_trade(d_rows.reshape(sources, capacity, width)).reshape(
        experts * capacity, width
    )
    back = returned[index].reshape(per_device, top, width)
    grad_h = flowing + jnp.sum(back.astype(jnp.float32), axis=1)
    grad_s = weights * (along - jnp.sum(weights * along, axis=1, keepdims=True))
    match = chosen[:, :, None] == labels[None, None, :]
    grad_logits = jnp.sum(jnp.where(match, grad_s[:, :, None], 0.0), axis=1).astype(jnp.bfloat16)
    local_router = contract_first(hidden, grad_logits)
    grad_h = grad_h + contract_last(grad_logits, router_layer)
    passed = grad_h.astype(jnp.bfloat16)
    grads = (
        contract_first(arrived, d_gate),
        contract_first(arrived, d_up),
        contract_first(inner, grad_rows),
    )
    return passed, grads, local_router


def shards(tokens, cotangent, routes, router, w_gate, w_up, w_down):
    sources = lax.axis_size("expert")
    groups = lax.axis_size("dp")
    section_id = lax.axis_index("section")
    batches, per_device, width = tokens.shape
    top = routes.shape[3]
    experts = router.shape[2]
    capacity = 3 * per_device * top // (2 * experts)
    shape = (experts, capacity, sources, width)
    layers = 2
    mine = section_id
    own = (router[0], w_gate[0, 0], w_up[0, 0], w_down[0, 0], fetch(routes[0], mine))
    other = swap((router[0], w_gate[0, 0], w_up[0, 0], w_down[0, 0], fetch(routes[0], 1 - mine)))
    params = [
        tuple(pick(section_id == layer, a, b) for a, b in zip(own, other)) for layer in range(layers)
    ]
    hidden = fetch(tokens, mine)
    outs = []
    saved = []
    for layer in range(layers):
        router_layer, gate_weight, up_weight, down_weight, chosen = params[layer]
        hidden, kept = layer_forward(
            hidden, chosen, router_layer, gate_weight, up_weight, down_weight, shape
        )
        outs.append(hidden)
        saved.append(kept)
    upstream = fetch(cotangent, mine)
    passed = [None] * layers
    grads = [None] * layers
    routers = [None] * layers
    for layer in reversed(range(layers)):
        router_layer, gate_weight, up_weight, down_weight, chosen = params[layer]
        upstream, grads[layer], routers[layer] = layer_backward(
            upstream, saved[layer], chosen, router_layer, gate_weight, up_weight, down_weight, shape
        )
        passed[layer] = upstream
    first = section_id == 0

    def place(values):
        held = pick(first, values[0], values[1])
        sent = swap(pick(first, values[1], values[0]))
        return jnp.stack([pick(first, held, sent), pick(first, sent, held)])

    out_block = place(outs)
    grad_block = place(passed)
    own_grads = tuple(pick(first, a, b) for a, b in zip(grads[0], grads[1]))
    sent_grads = swap(
        tuple(pick(first, b, a).astype(jnp.bfloat16) for a, b in zip(grads[0], grads[1]))
    )
    whole_gate, whole_up, whole_down = (
        a + b.astype(jnp.float32) for a, b in zip(own_grads, sent_grads)
    )
    sum_gate, sum_up, sum_down = group_reduce(whole_gate, whole_up, whole_down, groups)
    own_router = pick(first, routers[0], routers[1])
    sum_router = own_router + swap(pick(first, routers[1], routers[0]))
    sum_router = device_reduce(sum_router, sources * groups)
    expert_scale = 1.0 / math.sqrt(batches * groups * per_device * top)
    router_scale = 1.0 / math.sqrt(batches * per_device * sources * groups)
    return (
        out_block[None],
        grad_block[None],
        (sum_gate * expert_scale)[None, None],
        (sum_up * expert_scale)[None, None],
        (sum_down * expert_scale)[None, None],
        (sum_router * router_scale)[None],
    )


def solution(mesh):
    placed = (
        P(None, ("expert", "dp"), None),
        P(None, ("expert", "dp"), None),
        P("section", None, ("expert", "dp"), None),
        P("section", None, None),
        P("section", "expert", None, None),
        P("section", "expert", None, None),
        P("section", "expert", None, None),
    )
    return jax.shard_map(
        shards,
        mesh=mesh,
        in_specs=placed,
        out_specs=(
            P("section", None, ("expert", "dp"), None),
            P("section", None, ("expert", "dp"), None),
            P("section", "expert", "dp", None),
            P("section", "expert", "dp", None),
            P("section", "expert", "dp", None),
            P("section", None, None),
        ),
        check_vma=False,
    )
```

time: 808 us -> 473 us (0.59)
  the two profiles are of different devices: /device:TPU:32 before, /device:TPU:35 now
where the time goes in v2:
time: 473 us; the launch traced here: 464 us
  waiting for transfers between devices  210 us (44%)
  starting transfers between devices  92.9 us (20%)
  local copies, waits for them, and re-layouts  66.9 us (14%)
  other arithmetic  55 us (12%)
  matrix products  37.4 us (8%)
    all_to_all x8, waiting for transfers between devices, expert_trade(): lax.all_to_all(block, 'expert', split_axis=0, concat_axis=0, tiled=True)  165 us
    all_to_all x8, starting transfers between devices, expert_trade(): lax.all_to_all(block, 'expert', split_axis=0, concat_axis=0, tiled=True)  58.5 us
    all_to_all x1, waiting for transfers between devices, group_reduce(): traded = lax.all_to_all(stacked, 'dp', 0, 0, tiled=True)  37.7 us
    dot_general x8, matrix products, contract_last(): lax.dot_general(left, right, (((1,), (1,)), ((), ())), preferred_element_...  13.4 us
    dot_general x8, matrix products, contract_first(): lax.dot_general(left, right, (((0,), (0,)), ((), ())), preferred_element_...  11.2 us
    all_to_all x1, starting transfers between devices, device_reduce(): lax.all_to_all(spread, ('expert', 'dp'), 0, 0, tiled=True)  10.2 us
    all_to_all x1, starting transfers between devices, device_reduce(): traded = lax.all_to_all(chunks, ('expert', 'dp'), 0, 0, tiled=True)  10.1 us
  transfers between devices with their start and end apart: 22, of which 12 were waited for; matrix products, arithmetic and copies ran while one was open for 21% of the time, Pallas kernels for 0%

profile of v2, /device:TPU:35, one launch (start us, length us, event | category | flops | bytes accessed | tf_op | source)
XLA Modules:
  0.0 464.3 jit_solution(17629671441132749112)
XLA Ops:
  7.4 1.9 scatter_custom_fusion
  10.5 10.7 %all-to-all-start = ((bf16[32,12,1024]{2,1,0:T(8,128)(2,1)}), bf16[32,12,1024]{2,1,0:T(8,128)(2,1)}, u32[]{:S(2)}, u32[]{:S(2)}) async-start(bf16[32,12,1024]{2,1,0:T(8,128)(2,1)} %reshape.393), calls=%async_computation | async-start | bytes 2097152 | tf_op jit(solution)/shard_map/all_to_all | solution.py:46
  22.3 27.2 %all-to-all-done = bf16[32,12,1024]{2,1,0:T(8,128)(2,1)} async-done(((bf16[32,12,1024]{2,1,0:T(8,128)(2,1)}), bf16[32,12,1024]{2,1,0:T(8,128)(2,1)}, u32[]{:S(2)}, u32[]{:S(2)}) %all-to-all-start) | async-done | bytes 786464 | tf_op jit(solution)/shard_map/all_to_all | solution.py:46
  51.5 3.3 multiply_convert_fusion.7
  55.5 2.1 convolution_convert_fusion.1
  58.9 5.2 %all-to-all-start.1 = ((bf16[32,12,1024]{2,1,0:T(8,128)(2,1)}), bf16[32,12,1024]{2,1,0:T(8,128)(2,1)S(1)}, u32[]{:S(2)}, u32[]{:S(2)}) async-start(bf16[32,12,1024]{2,1,0:T(8,128)(2,1)} %reshape.395), calls=%async_computation.1 | async-start | bytes 2097152 | tf_op jit(solution)/shard_map/all_to_all | solution.py:46
  66.5 1.7 mul.239
  68.7 23.3 %all-to-all-done.1 = bf16[32,12,1024]{2,1,0:T(8,128)(2,1)S(1)} async-done(((bf16[32,12,1024]{2,1,0:T(8,128)(2,1)}), bf16[32,12,1024]{2,1,0:T(8,128)(2,1)S(1)}, u32[]{:S(2)}, u32[]{:S(2)}) %all-to-all-start.1) | async-done | bytes 786464 | tf_op jit(solution)/shard_map/all_to_all | solution.py:46
  92.2 2.0 gather_fusion
  94.2 1.8 reshape.412
  98.9 2.8 scatter_custom_fusion.2
  101.7 2.2 reshape.403
  103.9 5.3 %all-to-all-start.4 = ((bf16[32,12,1024]{2,1,0:T(8,128)(2,1)}), bf16[32,12,1024]{2,1,0:T(8,128)(2,1)S(1)}, u32[]{:S(2)}, u32[]{:S(2)}) async-start(bf16[32,12,1024]{2,1,0:T(8,128)(2,1)} %reshape.403), calls=%async_computation.4 | async-start | bytes 2097152 | tf_op jit(solution)/shard_map/all_to_all | solution.py:46
  110.2 2.0 reshape.461
  112.3 3.1 scatter_custom_fusion.1
  115.3 2.1 reshape.399
  117.5 17.8 %all-to-all-done.4 = bf16[32,12,1024]{2,1,0:T(8,128)(2,1)S(1)} async-done(((bf16[32,12,1024]{2,1,0:T(8,128)(2,1)}), bf16[32,12,1024]{2,1,0:T(8,128)(2,1)S(1)}, u32[]{:S(2)}, u32[]{:S(2)}) %all-to-all-start.4) | async-done | bytes 786464 | tf_op jit(solution)/shard_map/all_to_all | solution.py:46
  135.2 7.2 %all-to-all-start.2 = ((bf16[32,12,1024]{2,1,0:T(8,128)(2,1)}), bf16[32,12,1024]{2,1,0:T(8,128)(2,1)}, u32[]{:S(2)}, u32[]{:S(2)}) async-start(bf16[32,12,1024]{2,1,0:T(8,128)(2,1)} %reshape.399), calls=%async_computation.2 | async-start | bytes 2097152 | tf_op jit(solution)/shard_map/all_to_all | solution.py:46
  143.5 2.9 fusion.18
  146.5 22.1 %all-to-all-done.2 = bf16[32,12,1024]{2,1,0:T(8,128)(2,1)} async-done(((bf16[32,12,1024]{2,1,0:T(8,128)(2,1)}), bf16[32,12,1024]{2,1,0:T(8,128)(2,1)}, u32[]{:S(2)}, u32[]{:S(2)}) %all-to-all-start.2) | async-done | bytes 786464 | tf_op jit(solution)/shard_map/all_to_all | solution.py:46
  169.9 1.9 fusion.17
  174.3 2.7 convolution_convert_fusion
  177.1 2.1 reshape.401
  179.2 7.2 %all-to-all-start.3 = ((bf16[32,12,1024]{2,1,0:T(8,128)(2,1)}), bf16[32,12,1024]{2,1,0:T(8,128)(2,1)}, u32[]{:S(2)}, u32[]{:S(2)}) async-start(bf16[32,12,1024]{2,1,0:T(8,128)(2,1)} %reshape.401), calls=%async_computation.3 | async-start | bytes 2097152 | tf_op jit(solution)/shard_map/all_to_all | solution.py:46
  186.4 2.0 fusion.16
  190.0 2.2 reshape.405
  192.1 19.9 %all-to-all-done.3 = bf16[32,12,1024]{2,1,0:T(8,128)(2,1)} async-done(((bf16[32,12,1024]{2,1,0:T(8,128)(2,1)}), bf16[32,12,1024]{2,1,0:T(8,128)(2,1)}, u32[]{:S(2)}, u32[]{:S(2)}) %all-to-all-start.3) | async-done | bytes 786464 | tf_op jit(solution)/shard_map/all_to_all | solution.py:46
  212.0 7.7 %all-to-all-start.5 = ((bf16[32,12,1024]{2,1,0:T(8,128)(2,1)}), bf16[32,12,1024]{2,1,0:T(8,128)(2,1)}, u32[]{:S(2)}, u32[]{:S(2)}) async-start(bf16[32,12,1024]{2,1,0:T(8,128)(2,1)} %reshape.405), calls=%async_computation.5 | async-start | bytes 2097152 | tf_op jit(solution)/shard_map/all_to_all | solution.py:46
  221.1 2.0 gather_fusion.1
  223.1 1.7 reshape.413
  224.8 3.7 multiply_reduce_fusion.1
  230.7 14.9 %all-to-all-done.5 = bf16[32,12,1024]{2,1,0:T(8,128)(2,1)} async-done(((bf16[32,12,1024]{2,1,0:T(8,128)(2,1)}), bf16[32,12,1024]{2,1,0:T(8,128)(2,1)}, u32[]{:S(2)}, u32[]{:S(2)}) %all-to-all-start.5) | async-done | bytes 786464 | tf_op jit(solution)/shard_map/all_to_all | solution.py:46
  246.8 2.1 gather_fusion.2
  248.9 1.7 reshape.415
  250.6 2.1 reduce_sum.176
  258.7 3.2 collective-permute-start.10
  264.1 10.1 %all-to-all-start.9 = ((f32[128,1,256]{2,1,0:T(1,128)}), f32[128,1,256]{2,1,0:T(1,128)}, u32[]{:S(2)}, u32[]{:S(2)}) async-start(f32[128,1,256]{2,1,0:T(1,128)} %reshape.508), calls=%async_computation.9 | async-start | bytes 262144 | tf_op jit(solution)/shard_map/all_to_all | solution.py:75
  275.4 2.1 scatter_custom_fusion.3
  278.6 4.9 %all-to-all-done.9 = f32[128,1,256]{2,1,0:T(1,128)} async-done(((f32[128,1,256]{2,1,0:T(1,128)}), f32[128,1,256]{2,1,0:T(1,128)}, u32[]{:S(2)}, u32[]{:S(2)}) %all-to-all-start.9) | async-done | bytes 131104 | tf_op jit(solution)/shard_map/all_to_all | solution.py:75
  283.5 5.7 %all-to-all-start.6 = ((bf16[32,12,1024]{2,1,0:T(8,128)(2,1)}), bf16[32,12,1024]{2,1,0:T(8,128)(2,1)S(1)}, u32[]{:S(2)}, u32[]{:S(2)}) async-start(bf16[32,12,1024]{2,1,0:T(8,128)(2,1)} %reshape.407), calls=%async_computation.6 | async-start | bytes 2097152 | tf_op jit(solution)/shard_map/all_to_all | solution.py:46
  289.8 1.8 reduce.24
  292.9 22.4 %all-to-all-done.6 = bf16[32,12,1024]{2,1,0:T(8,128)(2,1)S(1)} async-done(((bf16[32,12,1024]{2,1,0:T(8,128)(2,1)}), bf16[32,12,1024]{2,1,0:T(8,128)(2,1)S(1)}, u32[]{:S(2)}, u32[]{:S(2)}) %all-to-all-start.6) | async-done | bytes 786464 | tf_op jit(solution)/shard_map/all_to_all | solution.py:46
  315.3 10.2 %all-to-all-start.10 = ((f32[128,1,256]{2,1,0:T(1,128)}), f32[128,1,256]{2,1,0:T(1,128)}, u32[]{:S(2)}, u32[]{:S(2)}) async-start(f32[128,1,256]{2,1,0:T(1,128)} %reshape.510), calls=%async_computation.10 | async-start | bytes 262144 | tf_op jit(solution)/shard_map/all_to_all | solution.py:78
  326.6 2.1 fusion.60
  328.7 2.5 select_convert_fusion
  331.2 1.7 collective-permute-start.9
  333.0 2.4 multiply_convert_fusion.3
  336.5 2.4 select_convert_fusion.1
  339.6 2.4 select_convert_fusion.2
  342.8 2.2 fusion.12
  346.8 2.5 add_convert_fusion
  349.3 2.2 stack_reshape.17
  351.5 2.5 add_convert_fusion.1
  354.1 2.1 stack_reshape.16
  356.1 2.5 add_convert_fusion.2
  358.7 2.1 stack_reshape.15
  360.8 9.5 %all-to-all-start.7 = ((bf16[32,12,1024]{2,1,0:T(8,128)(2,1)}), bf16[32,12,1024]{2,1,0:T(8,128)(2,1)S(1)}, u32[]{:S(2)}, u32[]{:S(2)}) async-start(bf16[32,12,1024]{2,1,0:T(8,128)(2,1)} %reshape.409), calls=%async_computation.7 | async-start | bytes 2097152 | tf_op jit(solution)/shard_map/all_to_all | solution.py:46
  370.3 9.4 %pad_maximum_fusion = bf16[4,3,131072]{2,1,0:T(4,128)(2,1)} fusion(bf16[4,1,131072]{2,1,0:T(2,128)(2,1)S(1)} %copy-done.4, bf16[4,1,131072]{2,1,0:T(2,128)(2,1)} %stack_reshape.16, bf16[4,1,131072]{2,1,0:T(2,128)(2,1)} %stack_reshape.15), kind=kLoop, calls=%fused_computation.9 | loop fusion | flops 9437184 | bytes 6291456 | tf_op jit(solution)/shard_map/stack | solution.py:59
  379.7 17.3 %all-to-all-done.7 = bf16[32,12,1024]{2,1,0:T(8,128)(2,1)S(1)} async-done(((bf16[32,12,1024]{2,1,0:T(8,128)(2,1)}), bf16[32,12,1024]{2,1,0:T(8,128)(2,1)S(1)}, u32[]{:S(2)}, u32[]{:S(2)}) %all-to-all-start.7) | async-done | bytes 786464 | tf_op jit(solution)/shard_map/all_to_all | solution.py:46
  397.0 4.8 %all-to-all-start.8 = ((bf16[4,3,131072]{2,1,0:T(4,128)(2,1)}), bf16[4,3,131072]{2,1,0:T(4,128)(2,1)}, u32[]{:S(2)}, u32[]{:S(2)}) async-start(bf16[4,3,131072]{2,1,0:T(4,128)(2,1)} %pad_maximum_fusion), calls=%async_computation.8 | async-start | bytes 8388608 | tf_op jit(solution)/shard_map/all_to_all | solution.py:62
  409.5 1.8 reduce.25
  413.3 37.7 %all-to-all-done.8 = bf16[4,3,131072]{2,1,0:T(4,128)(2,1)} async-done(((bf16[4,3,131072]{2,1,0:T(4,128)(2,1)}), bf16[4,3,131072]{2,1,0:T(4,128)(2,1)}, u32[]{:S(2)}, u32[]{:S(2)}) %all-to-all-start.8) | async-done | bytes 3145760 | tf_op jit(solution)/shard_map/all_to_all | solution.py:62
  451.0 4.7 %convert_reduce_fusion = f32[3,131072]{1,0:T(4,128)S(1)} fusion(bf16[4,3,131072]{2,1,0:T(4,128)(2,1)} %all-to-all-done.8), kind=kLoop, calls=%fused_computation.8 | loop fusion | flops 2752512 | bytes 4718592 | tf_op jit(solution)/shard_map/reduce_sum | solution.py:63
  455.7 5.6 %fusion.6 = (f32[131072]{0:T(1024)S(1)}, f32[131072]{0:T(1024)S(1)}, f32[131072]{0:T(1024)S(1)}) fusion(f32[3,131072]{1,0:T(4,128)S(1)} %convert_reduce_fusion), kind=kLoop, calls=%fused_computation.49 | loop fusion | flops 393216 | bytes 3145728 | tf_op jit(solution)/shard_map/mul | solution.py:230
  (219 shorter events, 60.4 us)
Async XLA Ops:
  0.6 2.9 copy-start.43
  1.4 2.2 collective-permute-start
  3.0 65.2 %copy-start.15 = (bf16[128,1024]{1,0:T(8,128)(2,1)}, bf16[128,1024]{1,0:T(8,128)(2,1)S(1)}, u32[]{:S(2)}) copy-start(bf16[128,1024]{1,0:T(8,128)(2,1)S(1)} %dynamic-slice_bitcast_fusion) | copy-start | bytes 786436
  3.6 64.9 %copy-start.36 = (s32[128,2]{0,1:T(2,128)}, s32[128,2]{0,1:T(2,128)S(1)}, u32[]{:S(2)}) copy-start(s32[128,2]{0,1:T(2,128)S(1)} %get-tuple-element.49) | copy-start | bytes 3076
  7.4 60.9 %copy-start.41 = (s32[256,1]{0,1:T(1,128)}, s32[256,1]{0,1:T(1,128)S(1)}, u32[]{:S(2)}) copy-start(s32[256,1]{0,1:T(1,128)S(1)} %get-tuple-element.65) | copy-start | bytes 3076
  9.3 11.9 %copy-start.9 = (bf16[1,1,1024,512]{3,2,1,0:T(8,128)(2,1)S(1)}, bf16[1,1,1024,512]{3,2,1,0:T(8,128)(2,1)}, u32[]{:S(2)}) copy-start(bf16[1,1,1024,512]{3,2,1,0:T(8,128)(2,1)} %param.11) | copy-start | bytes 3145732
  10.5 39.0 %all-to-all-start = ((bf16[32,12,1024]{2,1,0:T(8,128)(2,1)}), bf16[32,12,1024]{2,1,0:T(8,128)(2,1)}, u32[]{:S(2)}, u32[]{:S(2)}) async-start(bf16[32,12,1024]{2,1,0:T(8,128)(2,1)} %reshape.393), calls=%async_computation | async-start | bytes 2097152 | tf_op jit(solution)/shard_map/all_to_all | solution.py:46
  21.2 29.7 %collective-permute-start.2 = (bf16[1024,512]{1,0:T(8,128)(2,1)S(1)}, bf16[1024,512]{1,0:T(8,128)(2,1)S(1)}, u32[]{:S(2)}, u32[]{:S(2)}) collective-permute-start(bf16[1024,512]{1,0:T(8,128)(2,1)S(1)} %bitcast.183), channel_id=1, source_target_pairs={{0,128},{128,0},{1,129},{129,1},{2,130},{130,2},{3,131},{131,3},{4... | collective-permute-start | bytes 3145736 | tf_op jit(solution)/shard_map/ppermute | solution.py:82
  21.8 29.6 %collective-permute-start.3 = (bf16[1024,512]{1,0:T(8,128)(2,1)}, bf16[1024,512]{1,0:T(8,128)(2,1)}, u32[]{:S(2)}, u32[]{:S(2)}) collective-permute-start(bf16[1024,512]{1,0:T(8,128)(2,1)} %bitcast.8), channel_id=1, source_target_pairs={{0,128},{128,0},{1,129},{129,1},{2,130},{130,2},{3,131},{131,3},{4... | collective-permute-start | bytes 3145736 | tf_op jit(solution)/shard_map/ppermute | solution.py:82
  21.9 32.9 %collective-permute-start.4 = (bf16[512,1024]{1,0:T(8,128)(2,1)}, bf16[512,1024]{1,0:T(8,128)(2,1)}, u32[]{:S(2)}, u32[]{:S(2)}) collective-permute-start(bf16[512,1024]{1,0:T(8,128)(2,1)} %bitcast.9), channel_id=1, source_target_pairs={{0,128},{128,0},{1,129},{129,1},{2,130},{130,2},{3,131},{131,3},{4... | collective-permute-start | bytes 3145736 | tf_op jit(solution)/shard_map/ppermute | solution.py:82
  50.8 3.9 copy-start.5
  50.9 3.9 copy-start.11
  51.4 3.3 copy-start.44
  57.7 6.5 %copy-start.23 = (bf16[1,1024,32]{1,2,0:T(8,128)(2,1)S(1)}, bf16[1,1024,32]{1,2,0:T(8,128)(2,1)}, u32[]{:S(2)}) copy-start(bf16[1,1024,32]{1,2,0:T(8,128)(2,1)} %param.10) | copy-start | bytes 196612
  58.9 6.4 %copy-start.32 = (bf16[2,128,1024]{2,1,0:T(8,128)(2,1)S(1)}, bf16[2,128,1024]{2,1,0:T(8,128)(2,1)}, u32[]{:S(2)}) copy-start(bf16[2,128,1024]{2,1,0:T(8,128)(2,1)} %param.8) | copy-start | bytes 1572868
  58.9 33.1 %all-to-all-start.1 = ((bf16[32,12,1024]{2,1,0:T(8,128)(2,1)}), bf16[32,12,1024]{2,1,0:T(8,128)(2,1)S(1)}, u32[]{:S(2)}, u32[]{:S(2)}) async-start(bf16[32,12,1024]{2,1,0:T(8,128)(2,1)} %reshape.395), calls=%async_computation.1 | async-start | bytes 2097152 | tf_op jit(solution)/shard_map/all_to_all | solution.py:46
  64.1 4.1 collective-permute-start.1
  68.2 25.9 %copy-start.37 = (s32[1024]{0:T(1024)}, s32[1024]{0:T(1024)S(1)}, u32[]{:S(2)}) copy-start(s32[1024]{0:T(1024)S(1)} %pad_clamp_fusion.1) | copy-start | bytes 12292
  68.3 30.1 %copy-start.25 = (bf16[1024,32]{0,1:T(8,128)(2,1)}, bf16[1024,32]{0,1:T(8,128)(2,1)S(1)}, u32[]{:S(2)}) copy-start(bf16[1024,32]{0,1:T(8,128)(2,1)S(1)} %collective-permute-done.1) | copy-start | bytes 196612
  68.5 25.6 %copy-start.39 = (f32[128]{0:T(128)}, f32[128]{0:T(128)S(1)}, u32[]{:S(2)}) copy-start(f32[128]{0:T(128)S(1)} %exponential_reduce_fusion.1) | copy-start | bytes 1540
  68.7 27.3 %copy-start.29 = (f32[128,2]{1,0:T(8,128)}, f32[128,2]{1,0:T(8,128)S(1)}, u32[]{:S(2)}) copy-start(f32[128,2]{1,0:T(8,128)S(1)} %copy.67) | copy-start | bytes 3076
  94.2 4.7 %copy-start.19 = (f32[256,1024]{1,0:T(8,128)S(1)}, f32[256,1024]{1,0:T(8,128)}, u32[]{:S(2)}) copy-start(f32[256,1024]{1,0:T(8,128)} %mul.239) | copy-start | bytes 3145732
  98.6 5.3 %copy-start.40 = (f32[128]{0:T(128)}, f32[128]{0:T(128)S(1)}, u32[]{:S(2)}) copy-start(f32[128]{0:T(128)S(1)} %exponential_reduce_fusion) | copy-start | bytes 1540
  98.7 5.1 %copy-start.31 = (f32[128,2]{1,0:T(8,128)}, f32[128,2]{1,0:T(8,128)S(1)}, u32[]{:S(2)}) copy-start(f32[128,2]{1,0:T(8,128)S(1)} %copy.72) | copy-start | bytes 3076
  103.9 31.4 %all-to-all-start.4 = ((bf16[32,12,1024]{2,1,0:T(8,128)(2,1)}), bf16[32,12,1024]{2,1,0:T(8,128)(2,1)S(1)}, u32[]{:S(2)}, u32[]{:S(2)}) async-start(bf16[32,12,1024]{2,1,0:T(8,128)(2,1)} %reshape.403), calls=%async_computation.4 | async-start | bytes 2097152 | tf_op jit(solution)/shard_map/all_to_all | solution.py:46
  135.2 33.3 %all-to-all-start.2 = ((bf16[32,12,1024]{2,1,0:T(8,128)(2,1)}), bf16[32,12,1024]{2,1,0:T(8,128)(2,1)}, u32[]{:S(2)}, u32[]{:S(2)}) async-start(bf16[32,12,1024]{2,1,0:T(8,128)(2,1)} %reshape.399), calls=%async_computation.2 | async-start | bytes 2097152 | tf_op jit(solution)/shard_map/all_to_all | solution.py:46
  169.9 2.0 copy-start.12
  169.9 2.0 copy-start.46
  179.2 32.8 %all-to-all-start.3 = ((bf16[32,12,1024]{2,1,0:T(8,128)(2,1)}), bf16[32,12,1024]{2,1,0:T(8,128)(2,1)}, u32[]{:S(2)}, u32[]{:S(2)}) async-start(bf16[32,12,1024]{2,1,0:T(8,128)(2,1)} %reshape.401), calls=%async_computation.3 | async-start | bytes 2097152 | tf_op jit(solution)/shard_map/all_to_all | solution.py:46
  186.4 2.1 copy-start.13
  190.0 29.8 %copy-start.42 = (s32[256,1]{0,1:T(1,128)S(1)}, s32[256,1]{0,1:T(1,128)}, u32[]{:S(2)}) copy-start(s32[256,1]{0,1:T(1,128)} %get-tuple-element.64) | copy-start | bytes 3076
  212.0 33.5 %all-to-all-start.5 = ((bf16[32,12,1024]{2,1,0:T(8,128)(2,1)}), bf16[32,12,1024]{2,1,0:T(8,128)(2,1)}, u32[]{:S(2)}, u32[]{:S(2)}) async-start(bf16[32,12,1024]{2,1,0:T(8,128)(2,1)} %reshape.405), calls=%async_computation.5 | async-start | bytes 2097152 | tf_op jit(solution)/shard_map/all_to_all | solution.py:46
  219.8 3.3 copy-start.38
  252.8 5.6 %copy-start.16 = (bf16[128,1024]{1,0:T(8,128)(2,1)S(1)}, bf16[128,1024]{1,0:T(8,128)(2,1)}, u32[]{:S(2)}) copy-start(bf16[128,1024]{1,0:T(8,128)(2,1)} %copy-done.15) | copy-start | bytes 786436
  254.2 20.2 %copy-start.17 = (bf16[128,1024]{1,0:T(8,128)(2,1)}, bf16[128,1024]{1,0:T(8,128)(2,1)S(1)}, u32[]{:S(2)}) copy-start(bf16[128,1024]{1,0:T(8,128)(2,1)S(1)} %get-tuple-element.53) | copy-start | bytes 786436
  255.4 18.8 %copy-start.30 = (f32[128,2]{1,0:T(8,128)S(1)}, f32[128,2]{1,0:T(8,128)}, u32[]{:S(2)}) copy-start(f32[128,2]{1,0:T(8,128)} %copy-done.29) | copy-start | bytes 3076
  258.7 4.2 collective-permute-start.10
  264.1 19.5 %all-to-all-start.9 = ((f32[128,1,256]{2,1,0:T(1,128)}), f32[128,1,256]{2,1,0:T(1,128)}, u32[]{:S(2)}, u32[]{:S(2)}) async-start(f32[128,1,256]{2,1,0:T(1,128)} %reshape.508), calls=%async_computation.9 | async-start | bytes 262144 | tf_op jit(solution)/shard_map/all_to_all | solution.py:75
  283.5 31.8 %all-to-all-start.6 = ((bf16[32,12,1024]{2,1,0:T(8,128)(2,1)}), bf16[32,12,1024]{2,1,0:T(8,128)(2,1)S(1)}, u32[]{:S(2)}, u32[]{:S(2)}) async-start(bf16[32,12,1024]{2,1,0:T(8,128)(2,1)} %reshape.407), calls=%async_computation.6 | async-start | bytes 2097152 | tf_op jit(solution)/shard_map/all_to_all | solution.py:46
  315.3 45.5 %all-to-all-start.10 = ((f32[128,1,256]{2,1,0:T(1,128)}), f32[128,1,256]{2,1,0:T(1,128)}, u32[]{:S(2)}, u32[]{:S(2)}) async-start(f32[128,1,256]{2,1,0:T(1,128)} %reshape.510), calls=%async_computation.10 | async-start | bytes 262144 | tf_op jit(solution)/shard_map/all_to_all | solution.py:78
  326.6 2.1 copy-start.20
  326.6 2.1 copy-start.35
  328.7 4.3 copy-start.21
  328.7 4.3 copy-start.45
  328.7 4.3 copy-start.47
  331.2 15.5 %collective-permute-start.9 = (bf16[512,1024]{1,0:T(8,128)(2,1)}, bf16[512,1024]{1,0:T(8,128)(2,1)}, u32[]{:S(2)}, u32[]{:S(2)}) collective-permute-start(bf16[512,1024]{1,0:T(8,128)(2,1)} %get-tuple-element.56), channel_id=1, source_target_pairs={{0,128},{128,0},{1,129},{129,1},{2,130},{130,2},{3,131},{131,3},{4... | collective-permute-start | bytes 3145736 | tf_op jit(solution)/shard_map/ppermute | solution.py:82
  333.0 2.5 copy-start.6
  336.4 2.4 copy-start.2
  338.9 12.6 %collective-permute-start.8 = (bf16[1024,512]{1,0:T(8,128)(2,1)}, bf16[1024,512]{1,0:T(8,128)(2,1)}, u32[]{:S(2)}, u32[]{:S(2)}) collective-permute-start(bf16[1024,512]{1,0:T(8,128)(2,1)} %get-tuple-element.58), channel_id=1, source_target_pairs={{0,128},{128,0},{1,129},{129,1},{2,130},{130,2},{3,131},{131,3},{4... | collective-permute-start | bytes 3145736 | tf_op jit(solution)/shard_map/ppermute | solution.py:82
  339.6 2.5 copy-start
  342.1 2.9 copy-start.10
  342.1 2.9 copy-start.14
  342.1 14.0 %collective-permute-start.7 = (bf16[1024,512]{1,0:T(8,128)(2,1)}, bf16[1024,512]{1,0:T(8,128)(2,1)}, u32[]{:S(2)}, u32[]{:S(2)}) collective-permute-start(bf16[1024,512]{1,0:T(8,128)(2,1)} %get-tuple-element.60), channel_id=1, source_target_pairs={{0,128},{128,0},{1,129},{129,1},{2,130},{130,2},{3,131},{131,3},{4... | collective-permute-start | bytes 3145736 | tf_op jit(solution)/shard_map/ppermute | solution.py:82
  349.3 2.2 copy-start.3
  354.0 2.1 copy-start.1
  358.7 11.6 %copy-start.4 = (bf16[4,1,131072]{2,1,0:T(2,128)(2,1)S(1)}, bf16[4,1,131072]{2,1,0:T(2,128)(2,1)}, u32[]{:S(2)}) copy-start(bf16[4,1,131072]{2,1,0:T(2,128)(2,1)} %stack_reshape.17) | copy-start | bytes 3145732
  360.8 36.2 %all-to-all-start.7 = ((bf16[32,12,1024]{2,1,0:T(8,128)(2,1)}), bf16[32,12,1024]{2,1,0:T(8,128)(2,1)S(1)}, u32[]{:S(2)}, u32[]{:S(2)}) async-start(bf16[32,12,1024]{2,1,0:T(8,128)(2,1)} %reshape.409), calls=%async_computation.7 | async-start | bytes 2097152 | tf_op jit(solution)/shard_map/all_to_all | solution.py:46
  379.7 22.1 %copy-start.8 = (f32[128,1024]{1,0:T(8,128)S(1)}, f32[128,1024]{1,0:T(8,128)}, u32[]{:S(2)}) copy-start(f32[128,1024]{1,0:T(8,128)} %get-tuple-element.34) | copy-start | bytes 1572868
  397.0 54.0 %all-to-all-start.8 = ((bf16[4,3,131072]{2,1,0:T(4,128)(2,1)}), bf16[4,3,131072]{2,1,0:T(4,128)(2,1)}, u32[]{:S(2)}, u32[]{:S(2)}) async-start(bf16[4,3,131072]{2,1,0:T(4,128)(2,1)} %pad_maximum_fusion), calls=%async_computation.8 | async-start | bytes 8388608 | tf_op jit(solution)/shard_map/all_to_all | solution.py:62
  401.9 1.6 collective-permute-start.5
  405.9 2.0 copy-start.18
  405.9 2.7 copy-start.27
  405.9 2.7 copy-start.28
  408.2 4.2 collective-permute-start.6
  (6 other events, 7.3 us)

commit v3 on v2

--- a/solution.py
+++ b/solution.py
@@ -162,6 +162,70 @@
         contract_first(inner, grad_rows),
     )
     return passed, grads, local_router
+
+
+def both_trade(first, second, shape):
+    experts, capacity, sources, width = shape
+    joined = jnp.concatenate(
+        [first.reshape(experts, capacity, width), second.reshape(experts, capacity, width)], axis=1
+    )
+    traded = expert_trade(joined)
+    return (
+        traded[:, :capacity].reshape(sources * capacity, width),
+        traded[:, capacity:].reshape(sources * capacity, width),
+    )
+
+
+def last_layer(hidden, upstream, chosen, router_layer, gate_weight, up_weight, down_weight, shape):
+    experts, capacity, sources, width = shape
+    per_device = hidden.shape[0]
+    top = chosen.shape[1]
+    labels = jnp.arange(experts, dtype=jnp.int32)
+    weights = route_weights(hidden, chosen, router_layer)
+    index = slot_index(chosen, experts, capacity)
+    flowing = upstream.astype(jnp.float32)
+    grad_y = (
+        (weights[:, :, None] * flowing[:, None, :])
+        .astype(jnp.bfloat16)
+        .reshape(per_device * top, width)
+    )
+    spread = (
+        jnp.zeros((experts * capacity, width), jnp.bfloat16)
+        .at[index]
+        .set(jnp.repeat(hidden, top, axis=0))
+    )
+    grad_spread = jnp.zeros((experts * capacity, width), jnp.bfloat16).at[index].set(grad_y)
+    arrived, grad_rows = both_trade(spread, grad_spread, shape)
+    gate = jnp.dot(arrived, gate_weight, preferred_element_type=jnp.float32)
+    up_term = jnp.dot(arrived, up_weight, preferred_element_type=jnp.float32)
+    active = jax.nn.silu(gate)
+    inner = (active * up_term).astype(jnp.bfloat16)
+    produced = jnp.dot(inner, down_weight, preferred_element_type=jnp.float32).astype(jnp.bfloat16)
+    d_hidden = contract_last(grad_rows, down_weight)
+    sigma = jax.nn.sigmoid(gate)
+    d_gate = (d_hidden * up_term * sigma * (1.0 + gate * (1.0 - sigma))).astype(jnp.bfloat16)
+    d_up = (d_hidden * active).astype(jnp.bfloat16)
+    d_rows = (contract_last(d_gate, gate_weight) + contract_last(d_up, up_weight)).astype(
+        jnp.bfloat16
+    )
+    grads = (
+        contract_first(arrived, d_gate),
+        contract_first(arrived, d_up),
+        contract_first(inner, grad_rows),
+    )
+    returned, returned_grad = both_trade(produced, d_rows, shape)
+    picked = returned[index].reshape(per_device, top, width).astype(jnp.float32)
+    back = returned_grad[index].reshape(per_device, top, width)
+    blended = jnp.sum(weights[:, :, None] * picked, axis=1)
+    mixed = (hidden.astype(jnp.float32) + blended).astype(jnp.bfloat16)
+    along = jnp.sum(flowing[:, None, :] * picked, axis=2)
+    grad_h = flowing + jnp.sum(back.astype(jnp.float32), axis=1)
+    grad_s = weights * (along - jnp.sum(weights * along, axis=1, keepdims=True))
+    match = chosen[:, :, None] == labels[None, None, :]
+    grad_logits = jnp.sum(jnp.where(match, grad_s[:, :, None], 0.0), axis=1).astype(jnp.bfloat16)
+    local_router = contract_first(hidden, grad_logits)
+    grad_h = grad_h + contract_last(grad_logits, router_layer)
+    return mixed, grad_h.astype(jnp.bfloat16), grads, local_router
 
 
 def shards(tokens, cotangent, routes, router, w_gate, w_up, w_down):
@@ -180,26 +244,21 @@
     params = [
         tuple(pick(section_id == layer, a, b) for a, b in zip(own, other)) for layer in range(layers)
     ]
-    hidden = fetch(tokens, mine)
-    outs = []
-    saved = []
-    for layer in range(layers):
-        router_layer, gate_weight, up_weight, down_weight, chosen = params[layer]
-        hidden, kept = layer_forward(
-            hidden, chosen, router_layer, gate_weight, up_weight, down_weight, shape
-        )
-        outs.append(hidden)
-        saved.append(kept)
-    upstream = fetch(cotangent, mine)
-    passed = [None] * layers
-    grads = [None] * layers
-    routers = [None] * layers
-    for layer in reversed(range(layers)):
-        router_layer, gate_weight, up_weight, down_weight, chosen = params[layer]
-        upstream, grads[layer], routers[layer] = layer_backward(
-            upstream, saved[layer], chosen, router_layer, gate_weight, up_weight, down_weight, shape
-        )
-        passed[layer] = upstream
+    router_first, gate_first, up_first, down_first, chosen_first = params[0]
+    router_last, gate_last, up_last, down_last, chosen_last = params[1]
+    middle, kept = layer_forward(
+        fetch(tokens, mine), chosen_first, router_first, gate_first, up_first, down_first, shape
+    )
+    final, upstream, grads_last, router_grad_last = last_layer(
+        middle, fetch(cotangent, mine), chosen_last, router_last, gate_last, up_last, down_last, shape
+    )
+    passed_first, grads_first, router_grad_first = layer_backward(
+        upstream, kept, chosen_first, router_first, gate_first, up_first, down_first, shape
+    )
+    outs = (middle, final)
+    passed = (passed_first, upstream)
+    grads = (grads_first, grads_last)
+    routers = (router_grad_first, router_grad_last)
     first = section_id == 0
 
     def place(values):

time: 473 us -> 471 us (level)
  the two profiles are of different devices: /device:TPU:35 before, /device:TPU:32 now
where the time goes in v3:
time: 471 us; the launch traced here: 463 us
  waiting for transfers between devices  182 us (39%)
  local copies, waits for them, and re-layouts  73.8 us (16%)
  starting transfers between devices  63.5 us (13%)
  other arithmetic  59.2 us (13%)
  blocking collectives  44.7 us (9%)
  matrix products  36.9 us (8%)
    all_to_all x5, waiting for transfers between devices, expert_trade(): lax.all_to_all(block, 'expert', split_axis=0, concat_axis=0, tiled=True)  135 us
    all_to_all x1, blocking collectives, expert_trade(): lax.all_to_all(block, 'expert', split_axis=0, concat_axis=0, tiled=True)  44.7 us
    all_to_all x5, starting transfers between devices, expert_trade(): lax.all_to_all(block, 'expert', split_axis=0, concat_axis=0, tiled=True)  37.9 us
    all_to_all x1, waiting for transfers between devices, group_reduce(): traded = lax.all_to_all(stacked, 'dp', 0, 0, tiled=True)  37.8 us
    dot_general x8, matrix products, contract_last(): lax.dot_general(left, right, (((1,), (1,)), ((), ())), preferred_element_...  13.5 us
    dot_general x8, matrix products, contract_first(): lax.dot_general(left, right, (((0,), (0,)), ((), ())), preferred_element_...  10.9 us
    all_to_all x1, starting transfers between devices, device_reduce(): traded = lax.all_to_all(chunks, ('expert', 'dp'), 0, 0, tiled=True)  10.4 us
    another operation x1, other arithmetic, group_reduce(): jnp.stack([part.reshape(groups, -1) for part in (whole_gate, whole_up, wh...  9.45 us
  transfers between devices with their start and end apart: 19, of which 9 were waited for; matrix products, arithmetic and copies ran while one was open for 14% of the time, Pallas kernels for 0%

profile of v3, /device:TPU:32, one launch (start us, length us, event | category | flops | bytes accessed | tf_op | source)
XLA Modules:
  0.0 462.5 jit_solution(4618452211353256768)
XLA Ops:
  6.6 1.9 scatter_custom_fusion
  9.8 11.2 %all-to-all-start = ((bf16[32,12,1024]{2,1,0:T(8,128)(2,1)}), bf16[32,12,1024]{2,1,0:T(8,128)(2,1)}, u32[]{:S(2)}, u32[]{:S(2)}) async-start(bf16[32,12,1024]{2,1,0:T(8,128)(2,1)} %reshape.392), calls=%async_computation | async-start | bytes 2097152 | tf_op jit(solution)/shard_map/all_to_all | solution.py:46
  21.7 28.1 %all-to-all-done = bf16[32,12,1024]{2,1,0:T(8,128)(2,1)} async-done(((bf16[32,12,1024]{2,1,0:T(8,128)(2,1)}), bf16[32,12,1024]{2,1,0:T(8,128)(2,1)}, u32[]{:S(2)}, u32[]{:S(2)}) %all-to-all-start) | async-done | bytes 786464 | tf_op jit(solution)/shard_map/all_to_all | solution.py:46
  51.8 3.0 multiply_convert_fusion.7
  55.5 1.8 convolution_convert_fusion.1
  58.6 5.8 %all-to-all-start.1 = ((bf16[32,12,1024]{2,1,0:T(8,128)(2,1)}), bf16[32,12,1024]{2,1,0:T(8,128)(2,1)S(1)}, u32[]{:S(2)}, u32[]{:S(2)}) async-start(bf16[32,12,1024]{2,1,0:T(8,128)(2,1)} %reshape.394), calls=%async_computation.1 | async-start | bytes 2097152 | tf_op jit(solution)/shard_map/all_to_all | solution.py:46
  65.9 1.7 mul.234
  68.0 25.1 %all-to-all-done.1 = bf16[32,12,1024]{2,1,0:T(8,128)(2,1)S(1)} async-done(((bf16[32,12,1024]{2,1,0:T(8,128)(2,1)}), bf16[32,12,1024]{2,1,0:T(8,128)(2,1)S(1)}, u32[]{:S(2)}, u32[]{:S(2)}) %all-to-all-start.1) | async-done | bytes 786464 | tf_op jit(solution)/shard_map/all_to_all | solution.py:46
  93.3 2.0 gather_fusion
  95.2 1.8 reshape.411
  100.0 2.8 scatter_custom_fusion.2
  105.1 2.0 reshape.460
  107.1 3.1 scatter_custom_fusion.1
  110.2 2.1 reshape.398
  112.4 1.7 pad_maximum_fusion.1
  114.0 44.7 %all_to_all.45 = bf16[32,24,1024]{2,1,0:T(8,128)(2,1)S(1)} all-to-all(bf16[32,24,1024]{2,1,0:T(8,128)(2,1)S(1)} %pad_maximum_fusion.1), channel_id=1, replica_groups=mesh['section'=2,'expert'=32,'dp'=4] {'expert'}, dimensions={0} | all-to-all | bytes 3145728 | tf_op jit(solution)/shard_map/all_to_all | solution.py:46
  158.7 1.8 fusion.58
  161.9 2.1 reshape.402
  164.0 2.5 fusion.18
  167.0 3.1 multiply_convert_fusion.6
  171.0 3.0 convolution_convert_fusion
  174.0 2.1 reshape.401
  176.1 2.4 fusion.16
  178.5 1.6 add_convert_fusion.4
  180.1 2.2 reshape.403
  182.3 2.8 pad_maximum_fusion.2
  185.2 5.7 %all-to-all-start.3 = ((bf16[32,24,1024]{2,1,0:T(8,128)(2,1)}), bf16[32,24,1024]{2,1,0:T(8,128)(2,1)}, u32[]{:S(2)}, u32[]{:S(2)}) async-start(bf16[32,24,1024]{2,1,0:T(8,128)(2,1)} %pad_maximum_fusion.2), calls=%async_computation.3 | async-start | bytes 3145728 | tf_op jit(solution)/shard_map/all_to_all | solution.py:46
  190.8 37.6 %all-to-all-done.3 = bf16[32,24,1024]{2,1,0:T(8,128)(2,1)} async-done(((bf16[32,24,1024]{2,1,0:T(8,128)(2,1)}), bf16[32,24,1024]{2,1,0:T(8,128)(2,1)}, u32[]{:S(2)}, u32[]{:S(2)}) %all-to-all-start.3) | async-done | bytes 1572896 | tf_op jit(solution)/shard_map/all_to_all | solution.py:46
  228.4 3.4 fusion.57
  233.1 2.0 gather_fusion.2
  235.1 2.7 reshape.414
  239.1 2.0 gather_fusion.1
  241.0 2.8 reshape.413
  243.9 4.0 multiply_reduce_fusion.1
  250.1 2.1 reduce_sum.176
  252.2 1.5 fusion.59
  260.7 10.4 %all-to-all-start.7 = ((f32[128,1,256]{2,1,0:T(1,128)}), f32[128,1,256]{2,1,0:T(1,128)}, u32[]{:S(2)}, u32[]{:S(2)}) async-start(f32[128,1,256]{2,1,0:T(1,128)} %reshape.507), calls=%async_computation.7 | async-start | bytes 262144 | tf_op jit(solution)/shard_map/all_to_all | solution.py:75
  272.3 2.1 scatter_custom_fusion.3
  275.5 7.0 %all-to-all-done.7 = f32[128,1,256]{2,1,0:T(1,128)} async-done(((f32[128,1,256]{2,1,0:T(1,128)}), f32[128,1,256]{2,1,0:T(1,128)}, u32[]{:S(2)}, u32[]{:S(2)}) %all-to-all-start.7) | async-done | bytes 131104 | tf_op jit(solution)/shard_map/all_to_all | solution.py:75
  282.5 5.1 %all-to-all-start.4 = ((bf16[32,12,1024]{2,1,0:T(8,128)(2,1)}), bf16[32,12,1024]{2,1,0:T(8,128)(2,1)S(1)}, u32[]{:S(2)}, u32[]{:S(2)}) async-start(bf16[32,12,1024]{2,1,0:T(8,128)(2,1)} %reshape.406), calls=%async_computation.4 | async-start | bytes 2097152 | tf_op jit(solution)/shard_map/all_to_all | solution.py:46
  288.2 1.9 reduce.24
  291.3 23.9 %all-to-all-done.4 = bf16[32,12,1024]{2,1,0:T(8,128)(2,1)S(1)} async-done(((bf16[32,12,1024]{2,1,0:T(8,128)(2,1)}), bf16[32,12,1024]{2,1,0:T(8,128)(2,1)S(1)}, u32[]{:S(2)}, u32[]{:S(2)}) %all-to-all-start.4) | async-done | bytes 786464 | tf_op jit(solution)/shard_map/all_to_all | solution.py:46
  315.2 8.0 %all-to-all-start.8 = ((f32[128,1,256]{2,1,0:T(1,128)}), f32[128,1,256]{2,1,0:T(1,128)}, u32[]{:S(2)}, u32[]{:S(2)}) async-start(f32[128,1,256]{2,1,0:T(1,128)} %reshape.509), calls=%async_computation.8 | async-start | bytes 262144 | tf_op jit(solution)/shard_map/all_to_all | solution.py:78
  323.5 1.8 fusion.62
  325.4 2.8 multiply_convert_fusion.3
  330.2 2.4 select_convert_fusion
  332.6 2.4 select_convert_fusion.1
  335.5 2.5 select_convert_fusion.2
  338.2 2.0 fusion.12
  341.9 2.5 add_convert_fusion
  344.5 2.2 stack_reshape.17
  346.7 2.5 add_convert_fusion.1
  349.2 2.1 stack_reshape.16
  351.3 1.8 add_convert_fusion.2
  353.2 2.1 stack_reshape.15
  355.3 10.2 %all-to-all-start.5 = ((bf16[32,12,1024]{2,1,0:T(8,128)(2,1)}), bf16[32,12,1024]{2,1,0:T(8,128)(2,1)S(1)}, u32[]{:S(2)}, u32[]{:S(2)}) async-start(bf16[32,12,1024]{2,1,0:T(8,128)(2,1)} %reshape.408), calls=%async_computation.5 | async-start | bytes 2097152 | tf_op jit(solution)/shard_map/all_to_all | solution.py:46
  365.5 9.4 %pad_maximum_fusion = bf16[4,3,131072]{2,1,0:T(4,128)(2,1)} fusion(bf16[4,1,131072]{2,1,0:T(2,128)(2,1)S(1)} %copy-done.2, bf16[4,1,131072]{2,1,0:T(2,128)(2,1)} %stack_reshape.16, bf16[4,1,131072]{2,1,0:T(2,128)(2,1)} %stack_reshape.15), kind=kLoop, calls=%fused_computation.9 | loop fusion | flops 9437184 | bytes 6291456 | tf_op jit(solution)/shard_map/stack | solution.py:59
  374.9 20.2 %all-to-all-done.5 = bf16[32,12,1024]{2,1,0:T(8,128)(2,1)S(1)} async-done(((bf16[32,12,1024]{2,1,0:T(8,128)(2,1)}), bf16[32,12,1024]{2,1,0:T(8,128)(2,1)S(1)}, u32[]{:S(2)}, u32[]{:S(2)}) %all-to-all-start.5) | async-done | bytes 786464 | tf_op jit(solution)/shard_map/all_to_all | solution.py:46
  395.1 4.8 %all-to-all-start.6 = ((bf16[4,3,131072]{2,1,0:T(4,128)(2,1)}), bf16[4,3,131072]{2,1,0:T(4,128)(2,1)}, u32[]{:S(2)}, u32[]{:S(2)}) async-start(bf16[4,3,131072]{2,1,0:T(4,128)(2,1)} %pad_maximum_fusion), calls=%async_computation.6 | async-start | bytes 8388608 | tf_op jit(solution)/shard_map/all_to_all | solution.py:62
  400.1 1.5 collective-permute-done.5
  407.6 1.9 reduce.25
  411.4 37.8 %all-to-all-done.6 = bf16[4,3,131072]{2,1,0:T(4,128)(2,1)} async-done(((bf16[4,3,131072]{2,1,0:T(4,128)(2,1)}), bf16[4,3,131072]{2,1,0:T(4,128)(2,1)}, u32[]{:S(2)}, u32[]{:S(2)}) %all-to-all-start.6) | async-done | bytes 3145760 | tf_op jit(solution)/shard_map/all_to_all | solution.py:62
  449.2 4.7 %convert_reduce_fusion = f32[3,131072]{1,0:T(4,128)S(1)} fusion(bf16[4,3,131072]{2,1,0:T(4,128)(2,1)} %all-to-all-done.6), kind=kLoop, calls=%fused_computation.8 | loop fusion | flops 2752512 | bytes 4718592 | tf_op jit(solution)/shard_map/reduce_sum | solution.py:63
  453.9 5.6 %fusion.6 = (f32[131072]{0:T(1024)S(1)}, f32[131072]{0:T(1024)S(1)}, f32[131072]{0:T(1024)S(1)}) fusion(f32[3,131072]{1,0:T(4,128)S(1)} %convert_reduce_fusion), kind=kLoop, calls=%fused_computation.51 | loop fusion | flops 393216 | bytes 3145728 | tf_op jit(solution)/shard_map/mul | solution.py:289
  (212 shorter events, 52.7 us)
Async XLA Ops:
  0.6 2.2 copy-start.41
  1.4 1.5 collective-permute-start
  2.4 65.3 %copy-start.14 = (bf16[128,1024]{1,0:T(8,128)(2,1)}, bf16[128,1024]{1,0:T(8,128)(2,1)S(1)}, u32[]{:S(2)}) copy-start(bf16[128,1024]{1,0:T(8,128)(2,1)S(1)} %dynamic-slice_bitcast_fusion) | copy-start | bytes 786436
  2.9 64.9 %copy-start.35 = (s32[128,2]{0,1:T(2,128)}, s32[128,2]{0,1:T(2,128)S(1)}, u32[]{:S(2)}) copy-start(s32[128,2]{0,1:T(2,128)S(1)} %get-tuple-element.53) | copy-start | bytes 3076
  6.6 61.0 %copy-start.39 = (s32[256,1]{0,1:T(1,128)}, s32[256,1]{0,1:T(1,128)S(1)}, u32[]{:S(2)}) copy-start(s32[256,1]{0,1:T(1,128)S(1)} %get-tuple-element.69) | copy-start | bytes 3076
  8.6 12.5 %copy-start.7 = (bf16[1,1,1024,512]{3,2,1,0:T(8,128)(2,1)S(1)}, bf16[1,1,1024,512]{3,2,1,0:T(8,128)(2,1)}, u32[]{:S(2)}) copy-start(bf16[1,1,1024,512]{3,2,1,0:T(8,128)(2,1)} %param.11) | copy-start | bytes 3145732
  9.8 40.1 %all-to-all-start = ((bf16[32,12,1024]{2,1,0:T(8,128)(2,1)}), bf16[32,12,1024]{2,1,0:T(8,128)(2,1)}, u32[]{:S(2)}, u32[]{:S(2)}) async-start(bf16[32,12,1024]{2,1,0:T(8,128)(2,1)} %reshape.392), calls=%async_computation | async-start | bytes 2097152 | tf_op jit(solution)/shard_map/all_to_all | solution.py:46
  21.0 30.1 %collective-permute-start.2 = (bf16[1024,512]{1,0:T(8,128)(2,1)S(1)}, bf16[1024,512]{1,0:T(8,128)(2,1)S(1)}, u32[]{:S(2)}, u32[]{:S(2)}) collective-permute-start(bf16[1024,512]{1,0:T(8,128)(2,1)S(1)} %bitcast.187), channel_id=1, source_target_pairs={{0,128},{128,0},{1,129},{129,1},{2,130},{130,2},{3,131},{131,3},{4... | collective-permute-start | bytes 3145736 | tf_op jit(solution)/shard_map/ppermute | solution.py:82
  21.1 30.6 %collective-permute-start.3 = (bf16[1024,512]{1,0:T(8,128)(2,1)}, bf16[1024,512]{1,0:T(8,128)(2,1)}, u32[]{:S(2)}, u32[]{:S(2)}) collective-permute-start(bf16[1024,512]{1,0:T(8,128)(2,1)} %bitcast.8), channel_id=1, source_target_pairs={{0,128},{128,0},{1,129},{129,1},{2,130},{130,2},{3,131},{131,3},{4... | collective-permute-start | bytes 3145736 | tf_op jit(solution)/shard_map/ppermute | solution.py:82
  21.6 33.2 %collective-permute-start.4 = (bf16[512,1024]{1,0:T(8,128)(2,1)}, bf16[512,1024]{1,0:T(8,128)(2,1)}, u32[]{:S(2)}, u32[]{:S(2)}) collective-permute-start(bf16[512,1024]{1,0:T(8,128)(2,1)} %bitcast.9), channel_id=1, source_target_pairs={{0,128},{128,0},{1,129},{129,1},{2,130},{130,2},{3,131},{131,3},{4... | collective-permute-start | bytes 3145736 | tf_op jit(solution)/shard_map/ppermute | solution.py:82
  51.1 3.6 copy-start.3
  51.2 3.6 copy-start.9
  51.8 3.0 copy-start.42
  54.8 0.7 copy-start.32
  57.3 7.0 %copy-start.22 = (bf16[1,1024,32]{1,2,0:T(8,128)(2,1)S(1)}, bf16[1,1024,32]{1,2,0:T(8,128)(2,1)}, u32[]{:S(2)}) copy-start(bf16[1,1024,32]{1,2,0:T(8,128)(2,1)} %param.10) | copy-start | bytes 196612
  58.6 6.1 %copy-start.31 = (bf16[2,128,1024]{2,1,0:T(8,128)(2,1)S(1)}, bf16[2,128,1024]{2,1,0:T(8,128)(2,1)}, u32[]{:S(2)}) copy-start(bf16[2,128,1024]{2,1,0:T(8,128)(2,1)} %param.8) | copy-start | bytes 1572868
  58.6 34.5 %all-to-all-start.1 = ((bf16[32,12,1024]{2,1,0:T(8,128)(2,1)}), bf16[32,12,1024]{2,1,0:T(8,128)(2,1)S(1)}, u32[]{:S(2)}, u32[]{:S(2)}) async-start(bf16[32,12,1024]{2,1,0:T(8,128)(2,1)} %reshape.394), calls=%async_computation.1 | async-start | bytes 2097152 | tf_op jit(solution)/shard_map/all_to_all | solution.py:46
  64.3 3.3 collective-permute-start.1
  64.7 0.8 copy-start.5
  67.6 27.6 %copy-start.36 = (s32[1024]{0:T(1024)}, s32[1024]{0:T(1024)S(1)}, u32[]{:S(2)}) copy-start(s32[1024]{0:T(1024)S(1)} %pad_clamp_fusion.1) | copy-start | bytes 12292
  67.6 31.8 %copy-start.24 = (bf16[1024,32]{0,1:T(8,128)(2,1)}, bf16[1024,32]{0,1:T(8,128)(2,1)S(1)}, u32[]{:S(2)}) copy-start(bf16[1024,32]{0,1:T(8,128)(2,1)S(1)} %collective-permute-done.1) | copy-start | bytes 196612
  67.9 27.3 %copy-start.37 = (f32[128]{0:T(128)}, f32[128]{0:T(128)S(1)}, u32[]{:S(2)}) copy-start(f32[128]{0:T(128)S(1)} %exponential_reduce_fusion.1) | copy-start | bytes 1540
  68.0 29.0 %copy-start.28 = (f32[128,2]{1,0:T(8,128)}, f32[128,2]{1,0:T(8,128)S(1)}, u32[]{:S(2)}) copy-start(f32[128,2]{1,0:T(8,128)S(1)} %copy.67) | copy-start | bytes 3076
  95.2 4.7 %copy-start.18 = (f32[256,1024]{1,0:T(8,128)S(1)}, f32[256,1024]{1,0:T(8,128)}, u32[]{:S(2)}) copy-start(f32[256,1024]{1,0:T(8,128)} %mul.234) | copy-start | bytes 3145732
  99.7 5.4 %copy-start.38 = (f32[128]{0:T(128)}, f32[128]{0:T(128)S(1)}, u32[]{:S(2)}) copy-start(f32[128]{0:T(128)S(1)} %exponential_reduce_fusion) | copy-start | bytes 1540
  99.8 5.3 %copy-start.30 = (f32[128,2]{1,0:T(8,128)}, f32[128,2]{1,0:T(8,128)S(1)}, u32[]{:S(2)}) copy-start(f32[128,2]{1,0:T(8,128)S(1)} %copy.72) | copy-start | bytes 3076
  164.0 2.5 copy-start.10
  170.2 0.8 copy-start.33
  176.1 2.4 copy-start.11
  180.1 2.2 copy-start.13
  185.2 5.7 %copy-start.40 = (s32[256,1]{0,1:T(1,128)S(1)}, s32[256,1]{0,1:T(1,128)}, u32[]{:S(2)}) copy-start(s32[256,1]{0,1:T(1,128)} %get-tuple-element.68) | copy-start | bytes 3076
  185.2 43.2 %all-to-all-start.3 = ((bf16[32,24,1024]{2,1,0:T(8,128)(2,1)}), bf16[32,24,1024]{2,1,0:T(8,128)(2,1)}, u32[]{:S(2)}, u32[]{:S(2)}) async-start(bf16[32,24,1024]{2,1,0:T(8,128)(2,1)} %pad_maximum_fusion.2), calls=%async_computation.3 | async-start | bytes 3145728 | tf_op jit(solution)/shard_map/all_to_all | solution.py:46
  241.0 9.0 %copy-start.19 = (f32[128,2,1024]{2,1,0:T(2,128)S(1)}, f32[128,2,1024]{2,1,0:T(2,128)}, u32[]{:S(2)}) copy-start(f32[128,2,1024]{2,1,0:T(2,128)} %reshape.414) | copy-start | bytes 3145732
  252.2 5.6 %copy-start.15 = (bf16[128,1024]{1,0:T(8,128)(2,1)S(1)}, bf16[128,1024]{1,0:T(8,128)(2,1)}, u32[]{:S(2)}) copy-start(bf16[128,1024]{1,0:T(8,128)(2,1)} %copy-done.14) | copy-start | bytes 786436
  253.7 17.5 %copy-start.16 = (bf16[128,1024]{1,0:T(8,128)(2,1)}, bf16[128,1024]{1,0:T(8,128)(2,1)S(1)}, u32[]{:S(2)}) copy-start(bf16[128,1024]{1,0:T(8,128)(2,1)S(1)} %get-tuple-element.57) | copy-start | bytes 786436
  254.9 16.2 %copy-start.29 = (f32[128,2]{1,0:T(8,128)S(1)}, f32[128,2]{1,0:T(8,128)}, u32[]{:S(2)}) copy-start(f32[128,2]{1,0:T(8,128)} %copy-done.28) | copy-start | bytes 3076
  258.1 1.4 collective-permute-start.10
  260.7 21.8 %all-to-all-start.7 = ((f32[128,1,256]{2,1,0:T(1,128)}), f32[128,1,256]{2,1,0:T(1,128)}, u32[]{:S(2)}, u32[]{:S(2)}) async-start(f32[128,1,256]{2,1,0:T(1,128)} %reshape.507), calls=%async_computation.7 | async-start | bytes 262144 | tf_op jit(solution)/shard_map/all_to_all | solution.py:75
  282.5 32.7 %all-to-all-start.4 = ((bf16[32,12,1024]{2,1,0:T(8,128)(2,1)}), bf16[32,12,1024]{2,1,0:T(8,128)(2,1)S(1)}, u32[]{:S(2)}, u32[]{:S(2)}) async-start(bf16[32,12,1024]{2,1,0:T(8,128)(2,1)} %reshape.406), calls=%async_computation.4 | async-start | bytes 2097152 | tf_op jit(solution)/shard_map/all_to_all | solution.py:46
  315.2 40.0 %all-to-all-start.8 = ((f32[128,1,256]{2,1,0:T(1,128)}), f32[128,1,256]{2,1,0:T(1,128)}, u32[]{:S(2)}, u32[]{:S(2)}) async-start(f32[128,1,256]{2,1,0:T(1,128)} %reshape.509), calls=%async_computation.8 | async-start | bytes 262144 | tf_op jit(solution)/shard_map/all_to_all | solution.py:78
  323.5 1.9 copy-start.43
  323.5 1.9 copy-start.44
  325.3 4.4 copy-start
  325.3 2.8 copy-start.4
  328.9 1.1 copy-start.20
  328.9 1.2 copy-start.34
  330.2 2.4 copy-start.1
  330.2 2.4 copy-start.21
  332.6 9.3 %collective-permute-start.9 = (bf16[512,1024]{1,0:T(8,128)(2,1)}, bf16[512,1024]{1,0:T(8,128)(2,1)}, u32[]{:S(2)}, u32[]{:S(2)}) collective-permute-start(bf16[512,1024]{1,0:T(8,128)(2,1)} %get-tuple-element.60), channel_id=1, source_target_pairs={{0,128},{128,0},{1,129},{129,1},{2,130},{130,2},{3,131},{131,3},{4... | collective-permute-start | bytes 3145736 | tf_op jit(solution)/shard_map/ppermute | solution.py:82
  335.0 11.7 %collective-permute-start.8 = (bf16[1024,512]{1,0:T(8,128)(2,1)}, bf16[1024,512]{1,0:T(8,128)(2,1)}, u32[]{:S(2)}, u32[]{:S(2)}) collective-permute-start(bf16[1024,512]{1,0:T(8,128)(2,1)} %get-tuple-element.62), channel_id=1, source_target_pairs={{0,128},{128,0},{1,129},{129,1},{2,130},{130,2},{3,131},{131,3},{4... | collective-permute-start | bytes 3145736 | tf_op jit(solution)/shard_map/ppermute | solution.py:82
  338.0 2.2 copy-start.8
  338.0 2.2 copy-start.12
  338.0 13.4 %collective-permute-start.7 = (bf16[1024,512]{1,0:T(8,128)(2,1)}, bf16[1024,512]{1,0:T(8,128)(2,1)}, u32[]{:S(2)}, u32[]{:S(2)}) collective-permute-start(bf16[1024,512]{1,0:T(8,128)(2,1)} %get-tuple-element.64), channel_id=1, source_target_pairs={{0,128},{128,0},{1,129},{129,1},{2,130},{130,2},{3,131},{131,3},{4... | collective-permute-start | bytes 3145736 | tf_op jit(solution)/shard_map/ppermute | solution.py:82
  353.2 12.3 %copy-start.2 = (bf16[4,1,131072]{2,1,0:T(2,128)(2,1)S(1)}, bf16[4,1,131072]{2,1,0:T(2,128)(2,1)}, u32[]{:S(2)}) copy-start(bf16[4,1,131072]{2,1,0:T(2,128)(2,1)} %stack_reshape.17) | copy-start | bytes 3145732
  355.3 39.8 %all-to-all-start.5 = ((bf16[32,12,1024]{2,1,0:T(8,128)(2,1)}), bf16[32,12,1024]{2,1,0:T(8,128)(2,1)S(1)}, u32[]{:S(2)}, u32[]{:S(2)}) async-start(bf16[32,12,1024]{2,1,0:T(8,128)(2,1)} %reshape.408), calls=%async_computation.5 | async-start | bytes 2097152 | tf_op jit(solution)/shard_map/all_to_all | solution.py:46
  374.9 25.0 %copy-start.6 = (f32[128,1024]{1,0:T(8,128)S(1)}, f32[128,1024]{1,0:T(8,128)}, u32[]{:S(2)}) copy-start(f32[128,1024]{1,0:T(8,128)} %get-tuple-element.34) | copy-start | bytes 1572868
  395.1 54.1 %all-to-all-start.6 = ((bf16[4,3,131072]{2,1,0:T(4,128)(2,1)}), bf16[4,3,131072]{2,1,0:T(4,128)(2,1)}, u32[]{:S(2)}, u32[]{:S(2)}) async-start(bf16[4,3,131072]{2,1,0:T(4,128)(2,1)} %pad_maximum_fusion), calls=%async_computation.6 | async-start | bytes 8388608 | tf_op jit(solution)/shard_map/all_to_all | solution.py:62
  400.0 1.6 collective-permute-start.5
  404.0 2.0 copy-start.17
  404.0 2.0 copy-start.23
  404.0 2.0 copy-start.25
  404.0 2.7 copy-start.26
  404.0 2.7 copy-start.27
  406.3 4.3 collective-permute-start.6

commit v4 on v3

--- a/solution.py
+++ b/solution.py
@@ -55,18 +55,21 @@
     return lax.dynamic_update_index_in_dim(store, jnp.where(valid, value, previous), place, 0)
 
 
-def group_reduce(whole_gate, whole_up, whole_down, groups):
-    stacked = jnp.stack(
-        [part.reshape(groups, -1) for part in (whole_gate, whole_up, whole_down)], axis=1
-    ).astype(jnp.bfloat16)
+def group_reduce(whole_gate, whole_up, whole_down, rider, groups):
+    parts = [part.reshape(groups, -1).astype(jnp.bfloat16) for part in (whole_gate, whole_up, whole_down)]
+    spread = jnp.broadcast_to(rider.reshape(1, -1).astype(jnp.bfloat16), (groups, rider.size))
+    stacked = jnp.concatenate(parts + [spread], axis=1)
     traded = lax.all_to_all(stacked, "dp", 0, 0, tiled=True)
     summed = jnp.sum(traded.astype(jnp.float32), axis=0)
+    sizes = [part.shape[1] for part in parts]
+    cuts = [0, sizes[0], sizes[0] + sizes[1], sizes[0] + sizes[1] + sizes[2]]
     rows_gate = whole_gate.shape[0] // groups
     rows_down = whole_down.shape[0] // groups
     return (
-        summed[0].reshape(rows_gate, whole_gate.shape[1]),
-        summed[1].reshape(rows_gate, whole_up.shape[1]),
-        summed[2].reshape(rows_down, whole_down.shape[1]),
+        summed[cuts[0] : cuts[1]].reshape(rows_gate, whole_gate.shape[1]),
+        summed[cuts[1] : cuts[2]].reshape(rows_gate, whole_up.shape[1]),
+        summed[cuts[2] : cuts[3]].reshape(rows_down, whole_down.shape[1]),
+        summed[cuts[3] :].reshape(rider.shape),
     )
 
 
@@ -226,6 +229,65 @@
     local_router = contract_first(hidden, grad_logits)
     grad_h = grad_h + contract_last(grad_logits, router_layer)
     return mixed, grad_h.astype(jnp.bfloat16), grads, local_router
+
+
+def first_backward(upstream, saved, chosen, params, shape, router_last, first):
+    router_layer, gate_weight, up_weight, down_weight = params
+    experts, capacity, sources, width = shape
+    hidden, picked, arrived, weights, index = saved
+    per_device = hidden.shape[0]
+    top = chosen.shape[1]
+    labels = jnp.arange(experts, dtype=jnp.int32)
+    flowing = upstream.astype(jnp.float32)
+    along = jnp.sum(
+        flowing[:, None, :] * picked.reshape(per_device, top, width).astype(jnp.float32), axis=2
+    )
+    grad_s = weights * (along - jnp.sum(weights * along, axis=1, keepdims=True))
+    match = chosen[:, :, None] == labels[None, None, :]
+    grad_logits = jnp.sum(jnp.where(match, grad_s[:, :, None], 0.0), axis=1).astype(jnp.bfloat16)
+    local_router = contract_first(hidden, grad_logits)
+    router_sum = pick(first, local_router, router_last) + swap(
+        pick(first, router_last, local_router)
+    )
+    riders = router_sum.reshape(sources, -1, width).astype(jnp.bfloat16)
+    grad_y = (
+        (weights[:, :, None] * flowing[:, None, :])
+        .astype(jnp.bfloat16)
+        .reshape(per_device * top, width)
+    )
+    spread = jnp.zeros((experts * capacity, width), jnp.bfloat16).at[index].set(grad_y)
+    traded = expert_trade(
+        jnp.concatenate([spread.reshape(experts, capacity, width), riders], axis=1)
+    )
+    grad_rows = traded[:, :capacity].reshape(sources * capacity, width)
+    partial = jnp.sum(traded[:, capacity:].astype(jnp.float32), axis=0)
+    gate = jnp.dot(arrived, gate_weight, preferred_element_type=jnp.float32)
+    up_term = jnp.dot(arrived, up_weight, preferred_element_type=jnp.float32)
+    active = jax.nn.silu(gate)
+    inner = (active * up_term).astype(jnp.bfloat16)
+    d_hidden = contract_last(grad_rows, down_weight)
+    sigma = jax.nn.sigmoid(gate)
+    d_gate = (d_hidden * up_term * sigma * (1.0 + gate * (1.0 - sigma))).astype(jnp.bfloat16)
+    d_up = (d_hidden * active).astype(jnp.bfloat16)
+    d_rows = (contract_last(d_gate, gate_weight) + contract_last(d_up, up_weight)).astype(
+        jnp.bfloat16
+    )
+    back_riders = jnp.broadcast_to(partial.astype(jnp.bfloat16)[None], (sources,) + partial.shape)
+    returned_all = expert_trade(
+        jnp.concatenate([d_rows.reshape(sources, capacity, width), back_riders], axis=1)
+    )
+    returned = returned_all[:, :capacity].reshape(experts * capacity, width)
+    router_grad = returned_all[:, capacity:].astype(jnp.float32).reshape(router_sum.shape)
+    back = returned[index].reshape(per_device, top, width)
+    grad_h = flowing + jnp.sum(back.astype(jnp.float32), axis=1)
+    grad_h = grad_h + contract_last(grad_logits, router_layer)
+    passed = grad_h.astype(jnp.bfloat16)
+    grads = (
+        contract_first(arrived, d_gate),
+        contract_first(arrived, d_up),
+        contract_first(inner, grad_rows),
+    )
+    return passed, grads, router_grad
 
 
 def shards(tokens, cotangent, routes, router, w_gate, w_up, w_down):
@@ -252,14 +314,19 @@
     final, upstream, grads_last, router_grad_last = last_layer(
         middle, fetch(cotangent, mine), chosen_last, router_last, gate_last, up_last, down_last, shape
     )
-    passed_first, grads_first, router_grad_first = layer_backward(
-        upstream, kept, chosen_first, router_first, gate_first, up_first, down_first, shape
+    first = section_id == 0
+    passed_first, grads_first, router_grad = first_backward(
+        upstream,
+        kept,
+        chosen_first,
+        (router_first, gate_first, up_first, down_first),
+        shape,
+        router_grad_last,
+        first,
     )
     outs = (middle, final)
     passed = (passed_first, upstream)
     grads = (grads_first, grads_last)
-    routers = (router_grad_first, router_grad_last)
-    first = section_id == 0
 
     def place(values):
         held = pick(first, values[0], values[1])
@@ -275,10 +342,9 @@
     whole_gate, whole_up, whole_down = (
         a + b.astype(jnp.float32) for a, b in zip(own_grads, sent_grads)
     )
-    sum_gate, sum_up, sum_down = group_reduce(whole_gate, whole_up, whole_down, groups)
-    own_router = pick(first, routers[0], routers[1])
-    sum_router = own_router + swap(pick(first, routers[1], routers[0]))
-    sum_router = device_reduce(sum_router, sources * groups)
+    sum_gate, sum_up, sum_down, sum_router = group_reduce(
+        whole_gate, whole_up, whole_down, router_grad, groups
+    )
     expert_scale = 1.0 / math.sqrt(batches * groups * per_device * top)
     router_scale = 1.0 / math.sqrt(batches * per_device * sources * groups)
     return (

time: 471 us -> 447 us (0.949)
  waiting for transfers between devices: 182 us -> 128 us
  blocking collectives: 44.7 us -> 80.1 us
  starting transfers between devices: 63.5 us -> 38.2 us
  local copies, waits for them, and re-layouts: 73.8 us -> 87.8 us
  other arithmetic: 59.2 us -> 72.1 us
  matrix products: 36.9 us -> 30 us
    all_to_all x5 -> x4, waiting for transfers between devices: 135 us -> 95.8 us  [expert_trade(): lax.all_to_all(block, 'expert', split_axis=0, concat_axis=0, tiled=True)]
    all_to_all x1 -> x2, blocking collectives: 44.7 us -> 80.1 us  [expert_trade(): lax.all_to_all(block, 'expert', split_axis=0, concat_axis=0, tiled=True)]
    all_to_all x2 -> x0, starting transfers between devices: 18.4 us -> none  [the longest x1 10.4 us: device_reduce(): traded = lax.all_to_all(chunks, ('expert', 'dp'), 0, 0, tiled=True)]
    another operation x8 -> x4, other arithmetic: 17.6 us -> 1.26 us  [the longest x1 9.45 us: group_reduce(): jnp.stack([part.reshape(groups, -1) for part in (whole_gate, whole_up, wh...]
    unnamed x95 -> x108, local copies, waits for them, and re-layouts: 5.93 us -> 21.4 us
    reduce_sum x1, other arithmetic: 4.7 us -> 18.7 us  [group_reduce(): summed = jnp.sum(traded.astype(jnp.float32), axis=0)]
    all_to_all x2, other arithmetic: 3.77 us -> 17 us  [group_reduce(): traded = lax.all_to_all(stacked, 'dp', 0, 0, tiled=True)]
    all_to_all x5 -> x4, starting transfers between devices: 37.9 us -> 28.3 us  [expert_trade(): lax.all_to_all(block, 'expert', split_axis=0, concat_axis=0, tiled=True)]
  transfers between devices with their start and end apart: 19 -> 16, of which waited for: 9 -> 6; matrix products, arithmetic and copies ran while one was open for 14% -> 9% of each run, Pallas kernels for 0% -> 0%
where the time goes in v4:
time: 447 us; the launch traced here: 439 us
  waiting for transfers between devices  128 us (29%)
  local copies, waits for them, and re-layouts  87.8 us (20%)
  blocking collectives  80.1 us (18%)
  other arithmetic  72.1 us (16%)
  starting transfers between devices  38.2 us (9%)
  matrix products  30 us (7%)
    all_to_all x4, waiting for transfers between devices, expert_trade(): lax.all_to_all(block, 'expert', split_axis=0, concat_axis=0, tiled=True)  95.8 us
    all_to_all x2, blocking collectives, expert_trade(): lax.all_to_all(block, 'expert', split_axis=0, concat_axis=0, tiled=True)  80.1 us
    all_to_all x1, waiting for transfers between devices, group_reduce(): traded = lax.all_to_all(stacked, 'dp', 0, 0, tiled=True)  32.3 us
    all_to_all x4, starting transfers between devices, expert_trade(): lax.all_to_all(block, 'expert', split_axis=0, concat_axis=0, tiled=True)  28.3 us
    unnamed x108, local copies, waits for them, and re-layouts  21.4 us
    reduce_sum x1, other arithmetic, group_reduce(): summed = jnp.sum(traded.astype(jnp.float32), axis=0)  18.7 us
    all_to_all x2, other arithmetic, group_reduce(): traded = lax.all_to_all(stacked, 'dp', 0, 0, tiled=True)  17 us
    dot_general x8, matrix products, contract_first(): lax.dot_general(left, right, (((0,), (0,)), ((), ())), preferred_element_...  10.7 us
  transfers between devices with their start and end apart: 16, of which 6 were waited for; matrix products, arithmetic and copies ran while one was open for 9% of the time, Pallas kernels for 0%

profile of v4, /device:TPU:32, one launch (start us, length us, event | category | flops | bytes accessed | tf_op | source)
XLA Modules:
  0.0 438.7 jit_solution(10862140200363646804)
XLA Ops:
  6.6 1.9 scatter_custom_fusion
  9.7 11.2 %all-to-all-start = ((bf16[32,12,1024]{2,1,0:T(8,128)(2,1)}), bf16[32,12,1024]{2,1,0:T(8,128)(2,1)}, u32[]{:S(2)}, u32[]{:S(2)}) async-start(bf16[32,12,1024]{2,1,0:T(8,128)(2,1)} %reshape.423), calls=%async_computation | async-start | bytes 2097152 | tf_op jit(solution)/shard_map/all_to_all | solution.py:46
  21.7 28.1 %all-to-all-done = bf16[32,12,1024]{2,1,0:T(8,128)(2,1)} async-done(((bf16[32,12,1024]{2,1,0:T(8,128)(2,1)}), bf16[32,12,1024]{2,1,0:T(8,128)(2,1)}, u32[]{:S(2)}, u32[]{:S(2)}) %all-to-all-start) | async-done | bytes 786464 | tf_op jit(solution)/shard_map/all_to_all | solution.py:46
  49.8 1.3 reshape.424
  51.8 1.4 copy-done.23
  53.1 1.5 multiply_convert_fusion.7
  56.4 5.6 %all-to-all-start.1 = ((bf16[32,12,1024]{2,1,0:T(8,128)(2,1)}), bf16[32,12,1024]{2,1,0:T(8,128)(2,1)S(1)}, u32[]{:S(2)}, u32[]{:S(2)}) async-start(bf16[32,12,1024]{2,1,0:T(8,128)(2,1)} %reshape.425), calls=%async_computation.1 | async-start | bytes 2097152 | tf_op jit(solution)/shard_map/all_to_all | solution.py:46
  62.1 1.9 collective-permute-start.1
  64.0 1.4 mul.197
  65.4 1.9 mul.198
  69.0 22.2 %all-to-all-done.1 = bf16[32,12,1024]{2,1,0:T(8,128)(2,1)S(1)} async-done(((bf16[32,12,1024]{2,1,0:T(8,128)(2,1)}), bf16[32,12,1024]{2,1,0:T(8,128)(2,1)S(1)}, u32[]{:S(2)}, u32[]{:S(2)}) %all-to-all-start.1) | async-done | bytes 786464 | tf_op jit(solution)/shard_map/all_to_all | solution.py:46
  93.1 2.2 multiply_reduce_fusion.3
  98.0 2.8 scatter_custom_fusion.2
  103.3 3.1 scatter_custom_fusion.1
  106.4 2.1 reshape.429
  108.5 1.7 pad_maximum_fusion
  110.2 45.9 %all_to_all.39 = bf16[32,24,1024]{2,1,0:T(8,128)(2,1)S(1)} all-to-all(bf16[32,24,1024]{2,1,0:T(8,128)(2,1)S(1)} %pad_maximum_fusion), channel_id=1, replica_groups=mesh['section'=2,'expert'=32,'dp'=4] {'expert'}, dimensions={0} | all-to-all | bytes 3145728 | tf_op jit(solution)/shard_map/all_to_all | solution.py:46
  156.1 1.8 fusion.55
  157.9 1.3 reshape.431
  159.2 1.3 reshape.433
  160.5 2.5 fusion.15
  164.3 3.0 multiply_convert_fusion.6
  168.0 2.8 convolution_convert_fusion
  170.8 2.1 reshape.432
  172.9 2.3 fusion.13
  177.0 3.2 pad_maximum_fusion.1
  180.2 5.7 %all-to-all-start.3 = ((bf16[32,24,1024]{2,1,0:T(8,128)(2,1)}), bf16[32,24,1024]{2,1,0:T(8,128)(2,1)}, u32[]{:S(2)}, u32[]{:S(2)}) async-start(bf16[32,24,1024]{2,1,0:T(8,128)(2,1)} %pad_maximum_fusion.1), calls=%async_computation.3 | async-start | bytes 3145728 | tf_op jit(solution)/shard_map/all_to_all | solution.py:46
  186.5 35.2 %all-to-all-done.3 = bf16[32,24,1024]{2,1,0:T(8,128)(2,1)} async-done(((bf16[32,24,1024]{2,1,0:T(8,128)(2,1)}), bf16[32,24,1024]{2,1,0:T(8,128)(2,1)}, u32[]{:S(2)}, u32[]{:S(2)}) %all-to-all-start.3) | async-done | bytes 1572896 | tf_op jit(solution)/shard_map/all_to_all | solution.py:46
  221.7 3.4 fusion.54
  225.1 1.3 reshape.436
  226.4 2.1 gather_fusion.2
  228.5 2.7 reshape.444
  231.2 1.3 reshape.435
  232.5 2.1 gather_fusion.1
  234.6 2.7 reshape.443
  237.3 3.9 multiply_reduce_fusion.1
  241.3 2.5 reduce_sum.179
  246.7 1.7 mul.213
  248.4 3.3 scatter_custom_fusion.3
  253.7 34.3 %all_to_all.40 = bf16[32,13,1024]{2,1,0:T(8,128)(2,1)S(1)} all-to-all(bf16[32,13,1024]{2,1,0:T(8,128)(2,1)S(1)} %pad_maximum_fusion.2), channel_id=1, replica_groups=mesh['section'=2,'expert'=32,'dp'=4] {'expert'}, dimensions={0} | all-to-all | bytes 1703936 | tf_op jit(solution)/shard_map/all_to_all | solution.py:46
  288.2 2.1 fusion.59
  294.2 1.5 add_convert_fusion.3
  295.8 2.1 reshape.439
  299.2 2.6 pad_maximum_fusion.3
  301.8 5.7 %all-to-all-start.5 = ((bf16[32,13,1024]{2,1,0:T(8,128)(2,1)}), bf16[32,13,1024]{2,1,0:T(8,128)(2,1)}, u32[]{:S(2)}, u32[]{:S(2)}) async-start(bf16[32,13,1024]{2,1,0:T(8,128)(2,1)} %pad_maximum_fusion.3), calls=%async_computation.5 | async-start | bytes 2097152 | tf_op jit(solution)/shard_map/all_to_all | solution.py:46
  307.5 2.0 select_convert_fusion
  309.5 1.5 collective-permute-start.10
  311.0 2.4 select_convert_fusion.1
  314.4 2.4 select_convert_fusion.2
  318.2 1.7 convert_element_type.237
  319.9 1.8 add_convert_fusion.1
  321.8 1.8 convert_element_type.233
  323.6 1.8 add_convert_fusion.2
  325.4 1.8 convert_element_type.229
  327.2 10.3 %all-to-all-done.5 = bf16[32,13,1024]{2,1,0:T(8,128)(2,1)} async-done(((bf16[32,13,1024]{2,1,0:T(8,128)(2,1)}), bf16[32,13,1024]{2,1,0:T(8,128)(2,1)}, u32[]{:S(2)}, u32[]{:S(2)}) %all-to-all-start.5) | async-done | bytes 852000 | tf_op jit(solution)/shard_map/all_to_all | solution.py:46
  337.5 1.4 slice_reduce_fusion
  339.0 10.3 %maximum_bitcast_fusion = bf16[4,1,425984]{2,0,1:T(4,128)(2,1)S(1)} fusion(bf16[4,131072]{1,0:T(4,128)(2,1)} %convert_element_type.237, bf16[4,131072]{1,0:T(4,128)(2,1)} %convert_element_type.233, bf16[4,131072]{1,0:T(4,128)(2,1)} %convert_element_type.229, bf16[425984]{0:T(1024)(128)(2,1)S(1)} %pad.3.clone), kind=kLoop, calls=%fused_computation.9 | loop fusion | flops 13631488 | bytes 7405568 | tf_op jit(solution)/shard_map/all_to_all | solution.py:62
  349.8 6.7 %reduce.17 = bf16[4,425984]{1,0:T(4,128)(2,1)} reduce(bf16[4,1,425984]{2,0,1:T(4,128)(2,1)S(1)} %maximum_bitcast_fusion, bf16[]{:T(256)} %broadcast.231), dimensions={1}, to_apply=%copy.99.reduce_sub_computation | reduce | bytes 6815746 | tf_op jit(solution)/shard_map/all_to_all | solution.py:62
  356.5 7.1 %reshape.522 = bf16[4,2,212992]{2,1,0:T(2,128)(2,1)} reshape(bf16[4,425984]{1,0:T(4,128)(2,1)} %reduce.17) | data formatting | bytes 6815744
  363.6 4.8 %all-to-all-start.6 = ((bf16[4,2,212992]{2,1,0:T(2,128)(2,1)}), bf16[4,2,212992]{2,1,0:T(2,128)(2,1)}, u32[]{:S(2)}, u32[]{:S(2)}) async-start(bf16[4,2,212992]{2,1,0:T(2,128)(2,1)} %reshape.522), calls=%async_computation.6 | async-start | bytes 6815744 | tf_op jit(solution)/shard_map/all_to_all | solution.py:62
  369.2 1.5 reshape.440
  376.9 32.3 %all-to-all-done.6 = bf16[4,2,212992]{2,1,0:T(2,128)(2,1)} async-done(((bf16[4,2,212992]{2,1,0:T(2,128)(2,1)}), bf16[4,2,212992]{2,1,0:T(2,128)(2,1)}, u32[]{:S(2)}, u32[]{:S(2)}) %all-to-all-start.6) | async-done | bytes 3407904 | tf_op jit(solution)/shard_map/all_to_all | solution.py:62
  409.2 6.5 %reshape.523 = bf16[4,1,425984]{2,1,0:T(2,128)(2,1)} reshape(bf16[4,2,212992]{2,1,0:T(2,128)(2,1)} %all-to-all-done.6) | data formatting | bytes 6815744
  415.7 18.7 %convert_reduce_fusion = f32[425984]{0:T(1024)S(1)} fusion(bf16[4,1,425984]{2,1,0:T(2,128)(2,1)} %reshape.523), kind=kLoop, calls=%fused_computation.8 | loop fusion | flops 2981888 | bytes 5111808 | tf_op jit(solution)/shard_map/reduce_sum | solution.py:63
  (225 shorter events, 47.1 us)
Async XLA Ops:
  0.6 2.2 copy-start.45
  1.4 1.5 collective-permute-start
  2.4 7.4 %copy-start.18 = (bf16[128,1024]{1,0:T(8,128)(2,1)}, bf16[128,1024]{1,0:T(8,128)(2,1)S(1)}, u32[]{:S(2)}) copy-start(bf16[128,1024]{1,0:T(8,128)(2,1)S(1)} %dynamic-slice_bitcast_fusion) | copy-start | bytes 786436
  6.6 60.7 %copy-start.43 = (s32[256,1]{0,1:T(1,128)}, s32[256,1]{0,1:T(1,128)S(1)}, u32[]{:S(2)}) copy-start(s32[256,1]{0,1:T(1,128)S(1)} %get-tuple-element.75) | copy-start | bytes 3076
  8.5 12.4 %copy-start.10 = (bf16[1,1,1024,512]{3,2,1,0:T(8,128)(2,1)S(1)}, bf16[1,1,1024,512]{3,2,1,0:T(8,128)(2,1)}, u32[]{:S(2)}) copy-start(bf16[1,1,1024,512]{3,2,1,0:T(8,128)(2,1)} %param.11) | copy-start | bytes 3145732
  9.7 40.1 %all-to-all-start = ((bf16[32,12,1024]{2,1,0:T(8,128)(2,1)}), bf16[32,12,1024]{2,1,0:T(8,128)(2,1)}, u32[]{:S(2)}, u32[]{:S(2)}) async-start(bf16[32,12,1024]{2,1,0:T(8,128)(2,1)} %reshape.423), calls=%async_computation | async-start | bytes 2097152 | tf_op jit(solution)/shard_map/all_to_all | solution.py:46
  21.0 30.1 %collective-permute-start.2 = (bf16[1024,512]{1,0:T(8,128)(2,1)S(1)}, bf16[1024,512]{1,0:T(8,128)(2,1)S(1)}, u32[]{:S(2)}, u32[]{:S(2)}) collective-permute-start(bf16[1024,512]{1,0:T(8,128)(2,1)S(1)} %bitcast.191), channel_id=1, source_target_pairs={{0,128},{128,0},{1,129},{129,1},{2,130},{130,2},{3,131},{131,3},{4... | collective-permute-start | bytes 3145736 | tf_op jit(solution)/shard_map/ppermute | solution.py:85
  21.1 30.7 %collective-permute-start.3 = (bf16[1024,512]{1,0:T(8,128)(2,1)}, bf16[1024,512]{1,0:T(8,128)(2,1)}, u32[]{:S(2)}, u32[]{:S(2)}) collective-permute-start(bf16[1024,512]{1,0:T(8,128)(2,1)} %bitcast.192), channel_id=1, source_target_pairs={{0,128},{128,0},{1,129},{129,1},{2,130},{130,2},{3,131},{131,3},{4... | collective-permute-start | bytes 3145736 | tf_op jit(solution)/shard_map/ppermute | solution.py:85
  21.6 33.0 %collective-permute-start.4 = (bf16[512,1024]{1,0:T(8,128)(2,1)}, bf16[512,1024]{1,0:T(8,128)(2,1)}, u32[]{:S(2)}, u32[]{:S(2)}) collective-permute-start(bf16[512,1024]{1,0:T(8,128)(2,1)} %bitcast.204), channel_id=1, source_target_pairs={{0,128},{128,0},{1,129},{129,1},{2,130},{130,2},{3,131},{131,3},{4... | collective-permute-start | bytes 3145736 | tf_op jit(solution)/shard_map/ppermute | solution.py:85
  51.1 3.5 copy-start.5
  51.1 2.0 copy-start.23
  51.1 3.5 copy-start.14
  51.7 2.9 copy-start.49
  51.7 2.9 copy-start.46
  54.6 1.8 copy-start.35
  55.3 6.8 %copy-start.31 = (bf16[1,1024,32]{1,2,0:T(8,128)(2,1)S(1)}, bf16[1,1024,32]{1,2,0:T(8,128)(2,1)}, u32[]{:S(2)}) copy-start(bf16[1,1024,32]{1,2,0:T(8,128)(2,1)} %param.10) | copy-start | bytes 196612
  55.3 8.7 %copy-start.34 = (bf16[2,128,1024]{2,1,0:T(8,128)(2,1)S(1)}, bf16[2,128,1024]{2,1,0:T(8,128)(2,1)}, u32[]{:S(2)}) copy-start(bf16[2,128,1024]{2,1,0:T(8,128)(2,1)} %param.8) | copy-start | bytes 1572868
  56.4 34.7 %all-to-all-start.1 = ((bf16[32,12,1024]{2,1,0:T(8,128)(2,1)}), bf16[32,12,1024]{2,1,0:T(8,128)(2,1)S(1)}, u32[]{:S(2)}, u32[]{:S(2)}) async-start(bf16[32,12,1024]{2,1,0:T(8,128)(2,1)} %reshape.425), calls=%async_computation.1 | async-start | bytes 2097152 | tf_op jit(solution)/shard_map/all_to_all | solution.py:46
  62.1 5.3 %copy-start.19 = (bf16[128,1024]{1,0:T(8,128)(2,1)S(1)}, bf16[128,1024]{1,0:T(8,128)(2,1)}, u32[]{:S(2)}) copy-start(bf16[128,1024]{1,0:T(8,128)(2,1)} %copy-done.18) | copy-start | bytes 786436
  62.1 5.3 %collective-permute-start.1 = (bf16[1024,32]{0,1:T(8,128)(2,1)S(1)}, bf16[1024,32]{0,1:T(8,128)(2,1)S(1)}, u32[]{:S(2)}, u32[]{:S(2)}) collective-permute-start(bf16[1024,32]{0,1:T(8,128)(2,1)S(1)} %bitcast.193), channel_id=1, source_target_pairs={{0,128},{128,0},{1,129},{129,1},{2,130},{130,2},{3,131},{131,3},{4... | collective-permute-start | bytes 196616 | tf_op jit(solution)/shard_map/ppermute | solution.py:85
  67.3 25.1 %copy-start.38 = (s32[1024]{0:T(1024)}, s32[1024]{0:T(1024)S(1)}, u32[]{:S(2)}) copy-start(s32[1024]{0:T(1024)S(1)} %pad_clamp_fusion.1) | copy-start | bytes 12292
  96.4 149.6 %copy-start.3 = (bf16[128,1024]{1,0:T(8,128)(2,1)}, bf16[128,1024]{1,0:T(8,128)(2,1)S(1)}, u32[]{:S(2)}) copy-start(bf16[128,1024]{1,0:T(8,128)(2,1)S(1)} %add_convert_fusion.6) | copy-start | bytes 786436
  160.5 3.1 copy-start.26
  160.5 2.5 copy-start.11
  160.5 2.5 copy-start.15
  163.0 1.2 copy-start.24
  164.3 3.8 copy-start.47
  168.0 4.9 %copy-start.29 = (bf16[384,512]{1,0:T(8,128)(2,1)S(1)}, bf16[384,512]{1,0:T(8,128)(2,1)}, u32[]{:S(2)}) copy-start(bf16[384,512]{1,0:T(8,128)(2,1)} %get-tuple-element.51) | copy-start | bytes 1179652
  172.9 2.3 copy-start.12
  172.9 2.3 copy-start.16
  172.9 2.3 copy-start.27
  180.2 5.7 %copy-start.44 = (s32[256,1]{0,1:T(1,128)S(1)}, s32[256,1]{0,1:T(1,128)}, u32[]{:S(2)}) copy-start(s32[256,1]{0,1:T(1,128)} %get-tuple-element.74) | copy-start | bytes 3076
  180.2 41.5 %all-to-all-start.3 = ((bf16[32,24,1024]{2,1,0:T(8,128)(2,1)}), bf16[32,24,1024]{2,1,0:T(8,128)(2,1)}, u32[]{:S(2)}, u32[]{:S(2)}) async-start(bf16[32,24,1024]{2,1,0:T(8,128)(2,1)} %pad_maximum_fusion.1), calls=%async_computation.3 | async-start | bytes 3145728 | tf_op jit(solution)/shard_map/all_to_all | solution.py:46
  234.6 6.6 %copy-start.42 = (f32[128]{0:T(128)S(1)}, f32[128]{0:T(128)}, u32[]{:S(2)}) copy-start(f32[128]{0:T(128)} %copy-done.41) | copy-start | bytes 1540
  243.8 2.0 copy-start.40
  243.8 2.0 copy-start.20
  243.8 2.5 copy-start.32
  245.1 3.3 copy-start.21
  246.2 6.8 %collective-permute-start.6 = (f32[1024,32]{0,1:T(8,128)S(1)}, f32[1024,32]{0,1:T(8,128)S(1)}, u32[]{:S(2)}, u32[]{:S(2)}) collective-permute-start(f32[1024,32]{0,1:T(8,128)S(1)} %get-tuple-element.64), channel_id=1, source_target_pairs={{0,128},{128,0},{1,129},{129,1},{2,130},{130,2},{3,131},{131,3},{4... | collective-permute-start | bytes 393224 | tf_op jit(solution)/shard_map/ppermute | solution.py:85
  253.7 34.5 %copy-start.36 = (bf16[384,512]{1,0:T(8,128)(2,1)S(1)}, bf16[384,512]{1,0:T(8,128)(2,1)}, u32[]{:S(2)}) copy-start(bf16[384,512]{1,0:T(8,128)(2,1)} %copy-done.35) | copy-start | bytes 1179652
  288.0 2.3 copy-start.8
  288.2 2.1 copy-start.48
  288.2 2.1 copy-start.50
  288.2 2.4 copy-start.51
  290.5 1.1 copy-start.6
  291.4 1.3 copy-start.25
  292.7 1.2 copy-start.13
  292.7 1.5 copy-start.17
  301.8 35.7 %all-to-all-start.5 = ((bf16[32,13,1024]{2,1,0:T(8,128)(2,1)}), bf16[32,13,1024]{2,1,0:T(8,128)(2,1)}, u32[]{:S(2)}, u32[]{:S(2)}) async-start(bf16[32,13,1024]{2,1,0:T(8,128)(2,1)} %pad_maximum_fusion.3), calls=%async_computation.5 | async-start | bytes 2097152 | tf_op jit(solution)/shard_map/all_to_all | solution.py:46
  307.5 3.6 copy-start.30
  309.5 3.9 copy-start.7
  309.5 7.7 %collective-permute-start.10 = (bf16[512,1024]{1,0:T(8,128)(2,1)S(1)}, bf16[512,1024]{1,0:T(8,128)(2,1)S(1)}, u32[]{:S(2)}, u32[]{:S(2)}) collective-permute-start(bf16[512,1024]{1,0:T(8,128)(2,1)S(1)} %get-tuple-element.68), channel_id=1, source_target_pairs={{0,128},{128,0},{1,129},{129,1},{2,130},{130,2},{3,131},{131,3},{4... | collective-permute-start | bytes 3145736 | tf_op jit(solution)/shard_map/ppermute | solution.py:85
  313.4 1.0 copy-start.28
  313.4 6.5 %collective-permute-start.9 = (bf16[1024,512]{1,0:T(8,128)(2,1)}, bf16[1024,512]{1,0:T(8,128)(2,1)}, u32[]{:S(2)}, u32[]{:S(2)}) collective-permute-start(bf16[1024,512]{1,0:T(8,128)(2,1)} %get-tuple-element.70), channel_id=1, source_target_pairs={{0,128},{128,0},{1,129},{129,1},{2,130},{130,2},{3,131},{131,3},{4... | collective-permute-start | bytes 3145736 | tf_op jit(solution)/shard_map/ppermute | solution.py:85
  314.4 2.5 copy-start.1
  314.4 3.1 copy-start
  316.9 6.7 %collective-permute-start.8 = (bf16[1024,512]{1,0:T(8,128)(2,1)}, bf16[1024,512]{1,0:T(8,128)(2,1)}, u32[]{:S(2)}, u32[]{:S(2)}) collective-permute-start(bf16[1024,512]{1,0:T(8,128)(2,1)} %get-tuple-element.72), channel_id=1, source_target_pairs={{0,128},{128,0},{1,129},{129,1},{2,130},{130,2},{3,131},{131,3},{4... | collective-permute-start | bytes 3145736 | tf_op jit(solution)/shard_map/ppermute | solution.py:85
  321.8 1.8 copy-start.2
  363.6 4.8 %copy-start.4 = (bf16[128,1024]{1,0:T(8,128)(2,1)S(1)}, bf16[128,1024]{1,0:T(8,128)(2,1)}, u32[]{:S(2)}) copy-start(bf16[128,1024]{1,0:T(8,128)(2,1)} %copy-done.3) | copy-start | bytes 786436
  363.6 4.8 %copy-start.9 = (f32[128,1024]{1,0:T(8,128)S(1)}, f32[128,1024]{1,0:T(8,128)}, u32[]{:S(2)}) copy-start(f32[128,1024]{1,0:T(8,128)} %get-tuple-element.37) | copy-start | bytes 1572868
  363.6 45.6 %all-to-all-start.6 = ((bf16[4,2,212992]{2,1,0:T(2,128)(2,1)}), bf16[4,2,212992]{2,1,0:T(2,128)(2,1)}, u32[]{:S(2)}, u32[]{:S(2)}) async-start(bf16[4,2,212992]{2,1,0:T(2,128)(2,1)} %reshape.522), calls=%async_computation.6 | async-start | bytes 6815744 | tf_op jit(solution)/shard_map/all_to_all | solution.py:62
  369.2 5.6 %collective-permute-start.5 = (bf16[128,1024]{1,0:T(8,128)(2,1)}, bf16[128,1024]{1,0:T(8,128)(2,1)S(1)}, u32[]{:S(2)}, u32[]{:S(2)}) collective-permute-start(bf16[128,1024]{1,0:T(8,128)(2,1)} %broadcast_select_fusion.20), channel_id=1, source_target_pairs={{0,128},{128,0},{1,129},{129,1},{2,130},{130,2},{3,131},{131,3},{4... | collective-permute-start | bytes 786440 | tf_op jit(solution)/shard_map/ppermute | solution.py:85
  372.1 1.9 copy-start.22
  374.3 1.8 collective-permute-start.7
  (4 other events, 2.6 us)
